TPU v7x, 512 devices: a whole 4x8x8 slice. The times are simulated.
512 devices in a mesh: section: 32 (over y, x), ctx: 16 (over z, core).
Axes of the slice: x: 4, y: 8, z: 8, core: 2. Of those that a mesh axis runs over, the one named last changes fastest.
Arguments:
- queries: bfloat16 [32, 2048, 2048], P('section', 'ctx'), may hold values from -6 to 6
- key_states: bfloat16 [32, 2048, 2048], P('section', 'ctx'), may hold values from -6 to 6
- value_states: bfloat16 [32, 2048, 2048], P('section', 'ctx'), may hold values from -6 to 6
- upstream: bfloat16 [32, 2048, 2048], P('section', 'ctx'), may hold values from -6 to 6
- layout: int32 [32, 16, 16, 4], P('section', 'ctx'), may hold values from 0 to 15, as said below
- segments: int32 [32, 16], P('section'), may hold values from 0 to 4, never falling along the last dimension, each value on 1 to 8 neighbouring positions
Outputs:
- attended: bfloat16 [32, 2048, 2048], P('section', 'ctx')
- grad_queries: bfloat16 [32, 2048, 2048], P('section', 'ctx')
- grad_keys: bfloat16 [32, 2048, 2048], P('section', 'ctx')
- grad_values: bfloat16 [32, 2048, 2048], P('section', 'ctx')
Inputs may be any that keep to these rules, and one draw needn't show every extreme that they name: `layout`: for section s, head h and query block a the four entries are a, a - 1, a - 2 and a - 3 - r for some r from 0 to 12, each taken modulo 16; they are distinct.
All inputs are finite; a program needn't handle non-finite values.
Results may differ from a plain program's by a relative error of at most 0.04.
Values may be sent and summed in bfloat16 or wider, within the bound.
No kernel may reach another device: no remote copies, remote signals or barrier semaphores. Data moves between devices by JAX's collectives and lax.ppermute only.
A program may use at most 64 MiB of HBM per device.

v0:
```python
import functools
import math

import jax
import jax.numpy as jnp
from jax import lax
from jax.experimental import pallas as pl
from jax.experimental.pallas import tpu as pltpu
from jax.sharding import PartitionSpec as P

HEADS = 16
BLK = 128
SLOTS = 4


def passed_along(value, axis, steps):
    count = lax.axis_size(axis)
    pairs = [(source, (source + steps) % count) for source in range(count)]
    return lax.ppermute(value, axis, pairs)


def head_kernel(lay_ref, seg_ref, qkv_ref, grad_ref, out_ref, dk_acc, dv_acc):
    block_count = qkv_ref.shape[0]
    head_dim = qkv_ref.shape[-1]
    score_scale = 1.0 / math.sqrt(head_dim)
    dk_acc[...] = jnp.zeros_like(dk_acc)
    dv_acc[...] = jnp.zeros_like(dv_acc)
    row = lax.broadcasted_iota(jnp.int32, (BLK, BLK), 0)
    col = lax.broadcasted_iota(jnp.int32, (BLK, BLK), 1)

    def body(a, carry):
        q = qkv_ref[a, 0]
        g = grad_ref[a]
        seg_a = seg_ref[a]
        blocks = [lay_ref[a * SLOTS + j] for j in range(SLOTS)]
        key_rows = jnp.concatenate([qkv_ref[b, 1] for b in blocks], axis=0)
        value_rows = jnp.concatenate([qkv_ref[b, 2] for b in blocks], axis=0)
        masks = []
        for b in blocks:
            diag = (b == a).astype(jnp.int32)
            open_ = jnp.logical_and(b < a, seg_ref[b] == seg_a).astype(jnp.int32)
            limit = row * diag + (1 - diag) * (open_ * BLK - 1)
            masks.append(col <= limit)
        visible = jnp.concatenate(masks, axis=1)
        scores = lax.dot_general(
            q, key_rows, (((1,), (1,)), ((), ())), preferred_element_type=jnp.float32
        ) * score_scale
        scores = jnp.where(visible, scores, -jnp.inf)
        row_max = jnp.max(scores, axis=-1, keepdims=True)
        raised = jnp.exp(scores - row_max)
        weights = raised / jnp.sum(raised, axis=-1, keepdims=True)
        weights_low = weights.astype(jnp.bfloat16)
        attended = jnp.dot(
            weights_low, value_rows, preferred_element_type=jnp.float32
        ).astype(jnp.bfloat16)
        grad_weight = lax.dot_general(
            g, value_rows, (((1,), (1,)), ((), ())), preferred_element_type=jnp.float32
        )
        row_inner = jnp.sum(
            g.astype(jnp.float32) * attended.astype(jnp.float32), axis=-1, keepdims=True
        )
        grad_score = (weights * (grad_weight - row_inner)).astype(jnp.bfloat16)
        grad_query = jnp.dot(grad_score, key_rows, preferred_element_type=jnp.float32)
        out_ref[a, 0] = attended
        out_ref[a, 1] = (grad_query * score_scale).astype(jnp.bfloat16)
        grad_key_rows = lax.dot_general(
            grad_score, q, (((0,), (0,)), ((), ())), preferred_element_type=jnp.float32
        ) * score_scale
        grad_value_rows = lax.dot_general(
            weights_low, g, (((0,), (0,)), ((), ())), preferred_element_type=jnp.float32
        )
        for j, b in enumerate(blocks):
            dk_acc[b] += grad_key_rows[j * BLK:(j + 1) * BLK]
            dv_acc[b] += grad_value_rows[j * BLK:(j + 1) * BLK]
        return carry

    lax.fori_loop(0, block_count, body, 0)
    for b in range(block_count):
        out_ref[b, 2] = dk_acc[b].astype(jnp.bfloat16)
        out_ref[b, 3] = dv_acc[b].astype(jnp.bfloat16)


def head_pass(plan, documents, qkv, grad):
    block_count, _, rows, head_dim = qkv.shape
    flops = 6 * 2 * block_count * rows * SLOTS * rows * head_dim
    return pl.pallas_call(
        head_kernel,
        out_shape=jax.ShapeDtypeStruct((block_count, 4, rows, head_dim), jnp.bfloat16),
        in_specs=[
            pl.BlockSpec(memory_space=pltpu.SMEM),
            pl.BlockSpec(memory_space=pltpu.SMEM),
            pl.BlockSpec(memory_space=pltpu.VMEM),
            pl.BlockSpec(memory_space=pltpu.VMEM),
        ],
        out_specs=pl.BlockSpec(memory_space=pltpu.VMEM),
        scratch_shapes=[
            pltpu.VMEM((block_count, rows, head_dim), jnp.float32),
            pltpu.VMEM((block_count, rows, head_dim), jnp.float32),
        ],
        cost_estimate=pl.CostEstimate(
            flops=flops,
            transcendentals=block_count * rows * SLOTS * rows,
            bytes_accessed=2 * 8 * block_count * rows * head_dim,
        ),
    )(plan, documents, qkv, grad)


def local(queries, key_states, value_states, upstream, layout, segments):
    section_rows, tok_dev, feature_width = queries.shape
    head_dim = feature_width // HEADS

    def head_major(field):
        return field.reshape(tok_dev, HEADS, head_dim).transpose(1, 0, 2)

    arrived = passed_along(upstream, "section", -1)
    qkv = jnp.stack(
        [head_major(queries), head_major(key_states), head_major(value_states)], axis=1
    )
    qkv = lax.all_to_all(qkv, "ctx", 0, 0, tiled=True)
    grad = lax.all_to_all(head_major(arrived), "ctx", 0, 0, tiled=True)
    block_count = qkv.shape[0]
    plan = layout[0, 0].reshape(block_count * SLOTS)
    documents = segments[0]
    results = head_pass(plan, documents, qkv, grad)
    back = lax.all_to_all(results, "ctx", 0, 0, tiled=True)

    def merge_heads(i):
        return back[:, i].transpose(1, 0, 2).reshape(section_rows, tok_dev, feature_width)

    return tuple(merge_heads(i) for i in range(4))


def solution(mesh):
    placed = (
        P("section", "ctx", None),
        P("section", "ctx", None),
        P("section", "ctx", None),
        P("section", "ctx", None),
        P("section", "ctx", None, None),
        P("section", None),
    )
    return jax.shard_map(
        local,
        mesh=mesh,
        in_specs=placed,
        out_specs=(
            P("section", "ctx", None),
            P("section", "ctx", None),
            P("section", "ctx", None),
            P("section", "ctx", None),
        ),
        check_vma=False,
    )
```

profile of v0, /device:TPU:1, one launch (start us, length us, event | category | flops | bytes accessed | tf_op | source)
XLA Modules:
  0.0 171.4 jit_solution(13535577998272393734)
XLA Ops:
  0.6 1.4 copy.18
  2.0 8.1 %collective-permute-start = (bf16[1,128,2048]{1,2,0:T(8,128)(2,1)S(1)}, bf16[1,128,2048]{1,2,0:T(8,128)(2,1)S(1)}, u32[]{:S(2)}, u32[]{:S(2)}) collective-permute-start(bf16[1,128,2048]{1,2,0:T(8,128)(2,1)S(1)} %copy.18), channel_id=1, source_target_pairs={{0,496},{16,0},{32,16},{48,32},{64,48},{80,64},{96,80},{112,96},{1... | collective-permute-start | bytes 1572872 | tf_op jit(solution)/shard_map/ppermute | solution.py:19
  10.1 10.6 %collective-permute-done = bf16[1,128,2048]{1,2,0:T(8,128)(2,1)S(1)} collective-permute-done((bf16[1,128,2048]{1,2,0:T(8,128)(2,1)S(1)}, bf16[1,128,2048]{1,2,0:T(8,128)(2,1)S(1)}, u32[]{:S(2)}, u32[]{:S(2)}) %collective-permute-start) | collective-permute-done | bytes 524320 | tf_op jit(solution)/shard_map/ppermute | solution.py:19
  20.7 1.0 copy.19
  21.7 12.0 %all-to-all-start.1 = ((bf16[16,128,128]{2,1,0:T(8,128)(2,1)}), bf16[16,128,128]{2,1,0:T(8,128)(2,1)S(1)}, u32[]{:S(2)}, u32[]{:S(2)}) async-start(bf16[16,128,128]{2,1,0:T(8,128)(2,1)} %bitcast.11), calls=%async_computation.1 | async-start | bytes 1048576 | tf_op jit(solution)/shard_map/all_to_all | solution.py:120
  34.0 0.3 copy.13
  34.6 0.3 copy.15
  35.3 0.3 copy.17
  35.6 1.3 pad_maximum_fusion
  36.9 14.0 %all-to-all-done.1.grad_ref = bf16[16,128,128]{2,1,0:T(8,128)(2,1)S(1)} async-done(((bf16[16,128,128]{2,1,0:T(8,128)(2,1)}), bf16[16,128,128]{2,1,0:T(8,128)(2,1)S(1)}, u32[]{:S(2)}, u32[]{:S(2)}) %all-to-all-start.1) | async-done | bytes 524320 | tf_op jit(solution)/shard_map/all_to_all | solution.py:120
  50.9 0.8 copy-done.4
  51.7 3.6 %all-to-all-start = ((bf16[16,3,128,128]{3,2,1,0:T(8,128)(2,1)}), bf16[16,3,128,128]{3,2,1,0:T(8,128)(2,1)S(1)}, u32[]{:S(2)}, u32[]{:S(2)}) async-start(bf16[16,3,128,128]{3,2,1,0:T(8,128)(2,1)} %pad_maximum_fusion), calls=%async_computation | async-start | bytes 3145728 | tf_op jit(solution)/shard_map/all_to_all | solution.py:119
  55.4 0.6 reshape_squeeze.3.lay_ref
  56.0 37.1 %all-to-all-done.qkv_ref = bf16[16,3,128,128]{3,2,1,0:T(8,128)(2,1)S(1)} async-done(((bf16[16,3,128,128]{3,2,1,0:T(8,128)(2,1)}), bf16[16,3,128,128]{3,2,1,0:T(8,128)(2,1)S(1)}, u32[]{:S(2)}, u32[]{:S(2)}) %all-to-all-start) | async-done | bytes 1572896 | tf_op jit(solution)/shard_map/all_to_all | solution.py:119
  93.2 1.2 copy-done
  94.3 16.5 %shard_map.93 = bf16[16,4,128,128]{3,2,1,0:T(8,128)(2,1)} custom-call(s32[64]{0:T(128)} %reshape_squeeze.3.lay_ref, s32[16]{0:T(128)} %bitcast.48, bf16[16,3,128,128]{3,2,1,0:T(8,128)(2,1)} %copy-done, bf16[16,128,128]{2,1,0:T(8,128)(2,1)} %copy-done.4), custom_call_target="tpu_custom_call" | custom-call | flops 1610612736 | bytes 4194304 | tf_op jit(solution)/shard_map/pallas_call | solution.py:86
  110.8 55.1 %all_to_all.15 = bf16[16,4,128,128]{3,2,1,0:T(8,128)(2,1)S(1)} all-to-all(bf16[16,4,128,128]{3,2,1,0:T(8,128)(2,1)} %shard_map.93), channel_id=1, replica_groups=mesh['section'=32,'ctx'=16] {'ctx'}, dimensions={0} | all-to-all | bytes 4194304 | tf_op jit(solution)/shard_map/all_to_all | solution.py:125
  166.2 0.3 copy.23
  166.5 1.0 copy.27
  167.5 0.3 copy.22
  167.8 1.0 copy.26
  169.1 1.0 copy.25
  170.1 0.3 copy.20
  170.4 1.0 copy.24
  (16 shorter events, 1.6 us)
Async XLA Ops:
  0.6 33.1 %copy-start.1 = (bf16[1,128,2048]{2,1,0:T(8,128)(2,1)S(1)}, bf16[1,128,2048]{2,1,0:T(8,128)(2,1)}, u32[]{:S(2)}) copy-start(bf16[1,128,2048]{2,1,0:T(8,128)(2,1)} %param.6) | copy-start | bytes 1572868
  2.0 18.7 %collective-permute-start = (bf16[1,128,2048]{1,2,0:T(8,128)(2,1)S(1)}, bf16[1,128,2048]{1,2,0:T(8,128)(2,1)S(1)}, u32[]{:S(2)}, u32[]{:S(2)}) collective-permute-start(bf16[1,128,2048]{1,2,0:T(8,128)(2,1)S(1)} %copy.18), channel_id=1, source_target_pairs={{0,496},{16,0},{32,16},{48,32},{64,48},{80,64},{96,80},{112,96},{1... | collective-permute-start | bytes 1572872 | tf_op jit(solution)/shard_map/ppermute | solution.py:19
  21.7 12.6 %copy-start.2 = (bf16[1,128,2048]{2,1,0:T(8,128)(2,1)S(1)}, bf16[1,128,2048]{2,1,0:T(8,128)(2,1)}, u32[]{:S(2)}) copy-start(bf16[1,128,2048]{2,1,0:T(8,128)(2,1)} %param.7) | copy-start | bytes 1572868
  21.7 29.2 %all-to-all-start.1 = ((bf16[16,128,128]{2,1,0:T(8,128)(2,1)}), bf16[16,128,128]{2,1,0:T(8,128)(2,1)S(1)}, u32[]{:S(2)}, u32[]{:S(2)}) async-start(bf16[16,128,128]{2,1,0:T(8,128)(2,1)} %bitcast.11), calls=%async_computation.1 | async-start | bytes 1048576 | tf_op jit(solution)/shard_map/all_to_all | solution.py:120
  34.0 1.0 copy-start.3
  36.9 18.4 %copy-start.5 = (s32[1,1,16,4]{2,3,1,0:T(4,128)S(1)}, s32[1,1,16,4]{2,3,1,0:T(4,128)}, u32[]{:S(2)}) copy-start(s32[1,1,16,4]{2,3,1,0:T(4,128)} %param.10) | copy-start | bytes 772
  50.9 0.8 copy-start.4
  51.7 41.4 %all-to-all-start = ((bf16[16,3,128,128]{3,2,1,0:T(8,128)(2,1)}), bf16[16,3,128,128]{3,2,1,0:T(8,128)(2,1)S(1)}, u32[]{:S(2)}, u32[]{:S(2)}) async-start(bf16[16,3,128,128]{3,2,1,0:T(8,128)(2,1)} %pad_maximum_fusion), calls=%async_computation | async-start | bytes 3145728 | tf_op jit(solution)/shard_map/all_to_all | solution.py:119
  93.2 1.2 copy-start
where the time goes:
time: 172 us; the launch traced here: 171 us
  waiting for transfers between devices  61.7 us (36%)
  blocking collectives  55.1 us (32%)
  starting transfers between devices  23.7 us (14%)
  Pallas kernels  16.5 us (10%)
  local copies, waits for them, and re-layouts  12.3 us (7%)
    all_to_all x1, blocking collectives, local(): back = lax.all_to_all(results, 'ctx', 0, 0, tiled=True)  55.1 us
    all_to_all x1, waiting for transfers between devices, local(): qkv = lax.all_to_all(qkv, 'ctx', 0, 0, tiled=True)  37.1 us
    pallas_call x1, Pallas kernels, head_pass(): pl.pallas_call(head_kernel, out_shape=jax.ShapeDtypeStruct((block_count,...  16.5 us
    all_to_all x1, waiting for transfers between devices, local(): grad = lax.all_to_all(head_major(arrived), 'ctx', 0, 0, tiled=True)  14 us
    all_to_all x1, starting transfers between devices, local(): grad = lax.all_to_all(head_major(arrived), 'ctx', 0, 0, tiled=True)  12 us
    ppermute x1, waiting for transfers between devices, passed_along(): return lax.ppermute(value, axis, pairs)  10.6 us
    unnamed x21, local copies, waits for them, and re-layouts  8.46 us
    ppermute x1, starting transfers between devices, passed_along(): return lax.ppermute(value, axis, pairs)  8.11 us
  transfers between devices with their start and end apart: 3, of which 3 were waited for; matrix products, arithmetic and copies ran while one was open for 2% of the time, Pallas kernels for 0%

commit v1 on v0

v1 whole, which is shorter than its diff:
```python
import math

import jax
import jax.numpy as jnp
from jax import lax
from jax.experimental import pallas as pl
from jax.experimental.pallas import tpu as pltpu
from jax.sharding import PartitionSpec as P


HEADS = 16
BLK = 128
SLOTS = 4


def passed_along(value, axis, steps):
    count = lax.axis_size(axis)
    pairs = [(source, (source + steps) % count) for source in range(count)]
    return lax.ppermute(value, axis, pairs)


def key_rows_of(qkv_ref, blocks, which):
    return jnp.concatenate([qkv_ref[b, which] for b in blocks], axis=0)


def forward_kernel(lay_ref, seg_ref, qkv_ref, o_ref, w_ref):
    block_count = qkv_ref.shape[0]
    head_dim = qkv_ref.shape[-1]
    score_scale = 1.0 / math.sqrt(head_dim)
    row = lax.broadcasted_iota(jnp.int32, (BLK, BLK), 0)
    col = lax.broadcasted_iota(jnp.int32, (BLK, BLK), 1)

    def body(a, carry):
        q = qkv_ref[a, 0]
        seg_a = seg_ref[a]
        blocks = [lay_ref[a * SLOTS + j] for j in range(SLOTS)]
        key_rows = key_rows_of(qkv_ref, blocks, 1)
        value_rows = key_rows_of(qkv_ref, blocks, 2)
        masks = []
        for b in blocks:
            diag = (b == a).astype(jnp.int32)
            open_ = jnp.logical_and(b < a, seg_ref[b] == seg_a).astype(jnp.int32)
            limit = row * diag + (1 - diag) * (open_ * BLK - 1)
            masks.append(col <= limit)
        visible = jnp.concatenate(masks, axis=1)
        scores = lax.dot_general(
            q, key_rows, (((1,), (1,)), ((), ())), preferred_element_type=jnp.float32
        ) * score_scale
        scores = jnp.where(visible, scores, -jnp.inf)
        row_max = jnp.max(scores, axis=-1, keepdims=True)
        raised = jnp.exp(scores - row_max)
        weights = raised / jnp.sum(raised, axis=-1, keepdims=True)
        w_ref[a] = weights
        o_ref[a] = jnp.dot(
            weights.astype(jnp.bfloat16), value_rows, preferred_element_type=jnp.float32
        ).astype(jnp.bfloat16)
        return carry

    lax.fori_loop(0, block_count, body, 0)


def backward_kernel(lay_ref, qkv_ref, g_ref, o_ref, w_ref, out_ref, dk_acc, dv_acc):
    block_count = qkv_ref.shape[0]
    head_dim = qkv_ref.shape[-1]
    score_scale = 1.0 / math.sqrt(head_dim)
    dk_acc[...] = jnp.zeros_like(dk_acc)
    dv_acc[...] = jnp.zeros_like(dv_acc)

    def body(a, carry):
        q = qkv_ref[a, 0]
        g = g_ref[a]
        blocks = [lay_ref[a * SLOTS + j] for j in range(SLOTS)]
        key_rows = key_rows_of(qkv_ref, blocks, 1)
        value_rows = key_rows_of(qkv_ref, blocks, 2)
        weights = w_ref[a]
        weights_low = weights.astype(jnp.bfloat16)
        grad_weight = lax.dot_general(
            g, value_rows, (((1,), (1,)), ((), ())), preferred_element_type=jnp.float32
        )
        row_inner = jnp.sum(
            g.astype(jnp.float32) * o_ref[a].astype(jnp.float32), axis=-1, keepdims=True
        )
        grad_score = (weights * (grad_weight - row_inner)).astype(jnp.bfloat16)
        grad_query = jnp.dot(grad_score, key_rows, preferred_element_type=jnp.float32)
        out_ref[a, 0] = (grad_query * score_scale).astype(jnp.bfloat16)
        grad_key_rows = lax.dot_general(
            grad_score, q, (((0,), (0,)), ((), ())), preferred_element_type=jnp.float32
        ) * score_scale
        grad_value_rows = lax.dot_general(
            weights_low, g, (((0,), (0,)), ((), ())), preferred_element_type=jnp.float32
        )
        for j, b in enumerate(blocks):
            dk_acc[b] += grad_key_rows[j * BLK:(j + 1) * BLK]
            dv_acc[b] += grad_value_rows[j * BLK:(j + 1) * BLK]
        return carry

    lax.fori_loop(0, block_count, body, 0)
    for b in range(block_count):
        out_ref[b, 1] = dk_acc[b].astype(jnp.bfloat16)
        out_ref[b, 2] = dv_acc[b].astype(jnp.bfloat16)


def forward_pass(plan, documents, qkv):
    block_count, _, rows, head_dim = qkv.shape
    flops = 2 * 2 * block_count * rows * SLOTS * rows * head_dim
    return pl.pallas_call(
        forward_kernel,
        out_shape=[
            jax.ShapeDtypeStruct((block_count, rows, head_dim), jnp.bfloat16),
            jax.ShapeDtypeStruct((block_count, rows, SLOTS * rows), jnp.float32),
        ],
        in_specs=[
            pl.BlockSpec(memory_space=pltpu.SMEM),
            pl.BlockSpec(memory_space=pltpu.SMEM),
            pl.BlockSpec(memory_space=pltpu.VMEM),
        ],
        out_specs=[pl.BlockSpec(memory_space=pltpu.VMEM)] * 2,
        cost_estimate=pl.CostEstimate(
            flops=flops,
            transcendentals=block_count * rows * SLOTS * rows,
            bytes_accessed=2 * 4 * block_count * rows * head_dim
            + 4 * block_count * rows * SLOTS * rows,
        ),
    )(plan, documents, qkv)


def backward_pass(plan, qkv, grad, attended, weights):
    block_count, _, rows, head_dim = qkv.shape
    flops = 4 * 2 * block_count * rows * SLOTS * rows * head_dim
    return pl.pallas_call(
        backward_kernel,
        out_shape=jax.ShapeDtypeStruct((block_count, 3, rows, head_dim), jnp.bfloat16),
        in_specs=[pl.BlockSpec(memory_space=pltpu.SMEM)]
        + [pl.BlockSpec(memory_space=pltpu.VMEM)] * 4,
        out_specs=pl.BlockSpec(memory_space=pltpu.VMEM),
        scratch_shapes=[
            pltpu.VMEM((block_count, rows, head_dim), jnp.float32),
            pltpu.VMEM((block_count, rows, head_dim), jnp.float32),
        ],
        cost_estimate=pl.CostEstimate(
            flops=flops,
            transcendentals=0,
            bytes_accessed=2 * 9 * block_count * rows * head_dim
            + 4 * block_count * rows * SLOTS * rows,
        ),
    )(plan, qkv, grad, attended, weights)


def unshuffle_kernel(first_ref, rest_ref, *out_refs):
    head_count, _, head_dim = first_ref.shape
    for i, out_ref in enumerate(out_refs):
        for h in range(head_count):
            piece = first_ref[h] if i == 0 else rest_ref[h, i - 1]
            out_ref[0, :, h * head_dim:(h + 1) * head_dim] = piece


def unshuffle(first, rest, section_rows):
    head_count, arrays, rows, head_dim = rest.shape
    field = jax.ShapeDtypeStruct((section_rows, rows, head_count * head_dim), rest.dtype)
    return pl.pallas_call(
        unshuffle_kernel,
        out_shape=[field] * (arrays + 1),
        in_specs=[pl.BlockSpec(memory_space=pltpu.VMEM)] * 2,
        out_specs=[pl.BlockSpec(memory_space=pltpu.VMEM)] * (arrays + 1),
        cost_estimate=pl.CostEstimate(
            flops=0,
            transcendentals=0,
            bytes_accessed=4 * (first.size + rest.size),
        ),
    )(first, rest)


def local(queries, key_states, value_states, upstream, layout, segments):
    section_rows, tok_dev, feature_width = queries.shape
    head_dim = feature_width // HEADS

    def head_major(field):
        return field.reshape(tok_dev, HEADS, head_dim).transpose(1, 0, 2)

    fields = jnp.stack(
        [head_major(f) for f in (queries, key_states, value_states, upstream)], axis=1
    )
    fields = lax.all_to_all(fields, "ctx", 0, 0, tiled=True)
    block_count = fields.shape[0]
    plan = layout[0, 0].reshape(block_count * SLOTS)
    documents = segments[0]
    grad = passed_along(fields[:, 3], "section", -1)
    attended, weights = forward_pass(plan, documents, fields)
    attended_back = lax.all_to_all(attended, "ctx", 0, 0, tiled=True)
    results = backward_pass(plan, fields, grad, attended, weights)
    back = lax.all_to_all(results, "ctx", 0, 0, tiled=True)
    return tuple(unshuffle(attended_back, back, section_rows))


def solution(mesh):
    placed = (
        P("section", "ctx", None),
        P("section", "ctx", None),
        P("section", "ctx", None),
        P("section", "ctx", None),
        P("section", "ctx", None, None),
        P("section", None),
    )
    return jax.shard_map(
        local,
        mesh=mesh,
        in_specs=placed,
        out_specs=(
            P("section", "ctx", None),
            P("section", "ctx", None),
            P("section", "ctx", None),
            P("section", "ctx", None),
        ),
        check_vma=False,
    )
```

time: 172 us -> 172 us (level)
  Pallas kernels: 16.5 us -> 26.7 us
  blocking collectives: 55.1 us -> 47.6 us
  waiting for transfers between devices: 61.7 us -> 59.5 us
    pallas_call x1 -> x3, Pallas kernels: 16.5 us -> 26.7 us  [the longest x1 11.7 us: forward_pass(): pl.pallas_call(forward_kernel, out_shape=[jax.ShapeDtypeStruct((block_cou...]
    all_to_all x1, blocking collectives: 55.1 us -> 47.6 us  [local(): back = lax.all_to_all(results, 'ctx', 0, 0, tiled=True)]
    all_to_all x2, waiting for transfers between devices: 51.1 us -> 48.4 us  [the longest x1 48.4 us: local(): fields = lax.all_to_all(fields, 'ctx', 0, 0, tiled=True)]
    another operation x0 -> x1, local copies, waits for them, and re-layouts: none -> 2.61 us  [local(): jnp.stack([head_major(f) for f in (queries, key_states, value_states, ups...]
    reshape x4 -> x0, local copies, waits for them, and re-layouts: 1.86 us -> none  [head_major(): return field.reshape(tok_dev, HEADS, head_dim).transpose(1, 0, 2)]
    unnamed x21 -> x17, local copies, waits for them, and re-layouts: 8.46 us -> 6.92 us
  transfers between devices with their start and end apart: 3 -> 3, of which waited for: 3 -> 2; matrix products, arithmetic and copies ran while one was open for 2% -> 1% of each run, Pallas kernels for 0% -> 7%
where the time goes in v1:
time: 172 us; the launch traced here: 171 us
  waiting for transfers between devices  59.5 us (35%)
  blocking collectives  47.6 us (28%)
  Pallas kernels  26.7 us (16%)
  starting transfers between devices  24.1 us (14%)
  local copies, waits for them, and re-layouts  11.2 us (7%)
    all_to_all x1, waiting for transfers between devices, local(): fields = lax.all_to_all(fields, 'ctx', 0, 0, tiled=True)  48.4 us
    all_to_all x1, blocking collectives, local(): back = lax.all_to_all(results, 'ctx', 0, 0, tiled=True)  47.6 us
    all_to_all x1, starting transfers between devices, local(): fields = lax.all_to_all(fields, 'ctx', 0, 0, tiled=True)  12 us
    pallas_call x1, Pallas kernels, forward_pass(): pl.pallas_call(forward_kernel, out_shape=[jax.ShapeDtypeStruct((block_cou...  11.7 us
    pallas_call x1, Pallas kernels, backward_pass(): pl.pallas_call(backward_kernel, out_shape=jax.ShapeDtypeStruct((block_cou...  11.6 us
    ppermute x1, waiting for transfers between devices, passed_along(): return lax.ppermute(value, axis, pairs)  11.2 us
    ppermute x1, starting transfers between devices, passed_along(): return lax.ppermute(value, axis, pairs)  7.29 us
    unnamed x17, local copies, waits for them, and re-layouts  6.92 us
  transfers between devices with their start and end apart: 3, of which 2 were waited for; matrix products, arithmetic and copies ran while one was open for 1% of the time, Pallas kernels for 7%

profile of v1, /device:TPU:1, one launch (start us, length us, event | category | flops | bytes accessed | tf_op | source)
XLA Modules:
  0.0 171.2 jit_solution(8874742592668324861)
XLA Ops:
  0.6 0.0 copy-start.3
  0.7 1.4 copy.25
  2.1 1.3 copy.26
  3.4 0.0 copy-done.3
  3.4 1.0 copy.27
  4.4 1.0 copy.28
  5.4 1.5 pad_maximum_fusion
  6.8 2.6 %copy.29 = bf16[16,4,128,128]{3,2,1,0:T(8,128)(2,1)} copy(bf16[16,4,128,128]{2,3,0,1:T(8,128)(2,1)S(1)} %pad_maximum_fusion) | data formatting | bytes 4194304 | tf_op jit(solution)/shard_map/stack | solution.py:180
  9.5 12.0 %all-to-all-start = ((bf16[16,4,128,128]{3,2,1,0:T(8,128)(2,1)}), bf16[16,4,128,128]{3,2,1,0:T(8,128)(2,1)S(1)}, u32[]{:S(2)}, u32[]{:S(2)}) async-start(bf16[16,4,128,128]{3,2,1,0:T(8,128)(2,1)} %copy.29), calls=%async_computation | async-start | bytes 4194304 | tf_op jit(solution)/shard_map/all_to_all | solution.py:183
  21.4 0.1 copy.24
  21.5 0.6 reshape_squeeze.3.lay_ref
  22.1 48.4 %all-to-all-done.qkv_ref = bf16[16,4,128,128]{3,2,1,0:T(8,128)(2,1)S(1)} async-done(((bf16[16,4,128,128]{3,2,1,0:T(8,128)(2,1)}), bf16[16,4,128,128]{3,2,1,0:T(8,128)(2,1)S(1)}, u32[]{:S(2)}, u32[]{:S(2)}) %all-to-all-start) | async-done | bytes 2097184 | tf_op jit(solution)/shard_map/all_to_all | solution.py:183
  70.5 1.3 copy-done
  71.8 11.7 %shard_map.93 = (bf16[16,128,128]{2,1,0:T(8,128)(2,1)}, f32[16,128,512]{2,1,0:T(8,128)}) custom-call(s32[64]{0:T(128)} %reshape_squeeze.3.lay_ref, s32[16]{0:T(128)} %bitcast.31, bf16[16,4,128,128]{3,2,1,0:T(8,128)(2,1)} %copy-done), custom_call_target="tpu_custom_call" | custom-call | flops 536870912 | bytes 6291456 | tf_op jit(solution)/shard_map/pallas_call | solution.py:106
  83.5 4.8 %all-to-all-start.1 = ((bf16[16,128,128]{2,1,0:T(8,128)(2,1)}), bf16[16,128,128]{2,1,0:T(8,128)(2,1)S(1)}, u32[]{:S(2)}, u32[]{:S(2)}) async-start(bf16[16,128,128]{2,1,0:T(8,128)(2,1)} %get-tuple-element.6.o_ref), calls=%async_computation.1 | async-start | bytes 1048576 | tf_op jit(solution)/shard_map/all_to_all | solution.py:189
  88.3 1.1 slice_bitcast_fusion
  89.4 7.3 %collective-permute-start = (bf16[16,128,128]{2,1,0:T(8,128)(2,1)S(1)}, bf16[16,128,128]{2,1,0:T(8,128)(2,1)S(1)}, u32[]{:S(2)}, u32[]{:S(2)}) collective-permute-start(bf16[16,128,128]{2,1,0:T(8,128)(2,1)S(1)} %slice_bitcast_fusion), channel_id=1, source_target_pairs={{0,496},{16,0},{32,16},{48,32},{64,48},{80,64},{96,80},{112,96},{1... | collective-permute-start | bytes 1572872 | tf_op jit(solution)/shard_map/ppermute | solution.py:19
  96.7 11.2 %collective-permute-done.g_ref = bf16[16,128,128]{2,1,0:T(8,128)(2,1)S(1)} collective-permute-done((bf16[16,128,128]{2,1,0:T(8,128)(2,1)S(1)}, bf16[16,128,128]{2,1,0:T(8,128)(2,1)S(1)}, u32[]{:S(2)}, u32[]{:S(2)}) %collective-permute-start) | collective-permute-done | bytes 524320 | tf_op jit(solution)/shard_map/ppermute | solution.py:19
  107.9 0.8 copy-done.2
  108.6 11.6 %shard_map.94 = bf16[16,3,128,128]{3,2,1,0:T(8,128)(2,1)} custom-call(s32[64]{0:T(128)} %reshape_squeeze.3.lay_ref, bf16[16,4,128,128]{3,2,1,0:T(8,128)(2,1)} %copy-done, bf16[16,128,128]{2,1,0:T(8,128)(2,1)} %copy-done.2, bf16[16,128,128]{2,1,0:T(8,128)(2,1)} %get-tuple-element.6.o_ref, f32[16,128,512]{2,1,0:T(8,128)} %get-tuple-element.7.w_ref), custom_call_target="tpu_custom_call" | custom-call | flops 1073741824 | bytes 8912896 | tf_op jit(solution)/shard_map/pallas_call | solution.py:130
  120.2 0.0 all-to-all-done.1.first_ref
  120.2 47.6 %all_to_all.15.rest_ref = bf16[16,3,128,128]{3,2,1,0:T(8,128)(2,1)} all-to-all(bf16[16,3,128,128]{3,2,1,0:T(8,128)(2,1)} %shard_map.94), channel_id=1, replica_groups=mesh['section'=32,'ctx'=16] {'ctx'}, dimensions={0} | all-to-all | bytes 3145728 | tf_op jit(solution)/shard_map/all_to_all | solution.py:191
  167.8 0.0 copy-done.1
  167.8 3.4 %shard_map.95 = (bf16[1,128,2048]{2,1,0:T(8,128)(2,1)}, bf16[1,128,2048]{2,1,0:T(8,128)(2,1)}, bf16[1,128,2048]{2,1,0:T(8,128)(2,1)}, bf16[1,128,2048]{2,1,0:T(8,128)(2,1)}) custom-call(bf16[16,128,128]{2,1,0:T(8,128)(2,1)} %copy-done.1, bf16[16,3,128,128]{3,2,1,0:T(8,128)(2,1)} %all_to_all.15.rest_ref), custom_call_target="tpu_custom_call" | custom-call | bytes 4194304 | tf_op jit(solution)/shard_map/pallas_call | solution.py:160
  (7 shorter events, 0.0 us)
Async XLA Ops:
  0.6 2.7 %copy-start.3 = (bf16[1,128,2048]{2,1,0:T(8,128)(2,1)S(1)}, bf16[1,128,2048]{2,1,0:T(8,128)(2,1)}, u32[]{:S(2)}) copy-start(bf16[1,128,2048]{2,1,0:T(8,128)(2,1)} %param.8) | copy-start | bytes 1572868
  0.6 3.7 %copy-start.4 = (bf16[1,128,2048]{2,1,0:T(8,128)(2,1)S(1)}, bf16[1,128,2048]{2,1,0:T(8,128)(2,1)}, u32[]{:S(2)}) copy-start(bf16[1,128,2048]{2,1,0:T(8,128)(2,1)} %param.9) | copy-start | bytes 1572868
  9.5 12.0 %copy-start.5 = (s32[1,1,16,4]{2,3,1,0:T(4,128)S(1)}, s32[1,1,16,4]{2,3,1,0:T(4,128)}, u32[]{:S(2)}) copy-start(s32[1,1,16,4]{2,3,1,0:T(4,128)} %param.10) | copy-start | bytes 772
  9.5 61.0 %all-to-all-start = ((bf16[16,4,128,128]{3,2,1,0:T(8,128)(2,1)}), bf16[16,4,128,128]{3,2,1,0:T(8,128)(2,1)S(1)}, u32[]{:S(2)}, u32[]{:S(2)}) async-start(bf16[16,4,128,128]{3,2,1,0:T(8,128)(2,1)} %copy.29), calls=%async_computation | async-start | bytes 4194304 | tf_op jit(solution)/shard_map/all_to_all | solution.py:183
  70.5 1.3 copy-start
  83.5 36.8 %all-to-all-start.1 = ((bf16[16,128,128]{2,1,0:T(8,128)(2,1)}), bf16[16,128,128]{2,1,0:T(8,128)(2,1)S(1)}, u32[]{:S(2)}, u32[]{:S(2)}) async-start(bf16[16,128,128]{2,1,0:T(8,128)(2,1)} %get-tuple-element.6.o_ref), calls=%async_computation.1 | async-start | bytes 1048576 | tf_op jit(solution)/shard_map/all_to_all | solution.py:189
  89.4 18.5 %collective-permute-start = (bf16[16,128,128]{2,1,0:T(8,128)(2,1)S(1)}, bf16[16,128,128]{2,1,0:T(8,128)(2,1)S(1)}, u32[]{:S(2)}, u32[]{:S(2)}) collective-permute-start(bf16[16,128,128]{2,1,0:T(8,128)(2,1)S(1)} %slice_bitcast_fusion), channel_id=1, source_target_pairs={{0,496},{16,0},{32,16},{48,32},{64,48},{80,64},{96,80},{112,96},{1... | collective-permute-start | bytes 1572872 | tf_op jit(solution)/shard_map/ppermute | solution.py:19
  107.9 0.8 copy-start.2
  120.2 47.6 %copy-start.1 = (bf16[16,128,128]{2,1,0:T(8,128)(2,1)}, bf16[16,128,128]{2,1,0:T(8,128)(2,1)S(1)}, u32[]{:S(2)}) copy-start(bf16[16,128,128]{2,1,0:T(8,128)(2,1)S(1)} %all-to-all-done.1.first_ref) | copy-start | bytes 1572868

commit v2 on v1

--- a/solution.py
+++ b/solution.py
@@ -56,7 +56,7 @@
         ).astype(jnp.bfloat16)
         return carry
 
-    lax.fori_loop(0, block_count, body, 0)
+    lax.fori_loop(0, block_count, body, 0, unroll=4)
 
 
 def backward_kernel(lay_ref, qkv_ref, g_ref, o_ref, w_ref, out_ref, dk_acc, dv_acc):
@@ -94,7 +94,7 @@
             dv_acc[b] += grad_value_rows[j * BLK:(j + 1) * BLK]
         return carry
 
-    lax.fori_loop(0, block_count, body, 0)
+    lax.fori_loop(0, block_count, body, 0, unroll=4)
     for b in range(block_count):
         out_ref[b, 1] = dk_acc[b].astype(jnp.bfloat16)
         out_ref[b, 2] = dv_acc[b].astype(jnp.bfloat16)
@@ -146,6 +146,32 @@
     )(plan, qkv, grad, attended, weights)
 
 
+def shuffle_kernel(*refs):
+    *in_refs, out_ref = refs
+    head_count = out_ref.shape[0]
+    head_dim = out_ref.shape[-1]
+    for i, in_ref in enumerate(in_refs):
+        for h in range(head_count):
+            out_ref[h, i] = in_ref[0, :, h * head_dim:(h + 1) * head_dim]
+
+
+def shuffle(fields, head_count):
+    _, rows, width = fields[0].shape
+    head_dim = width // head_count
+    out = jax.ShapeDtypeStruct((head_count, len(fields), rows, head_dim), fields[0].dtype)
+    return pl.pallas_call(
+        shuffle_kernel,
+        out_shape=out,
+        in_specs=[pl.BlockSpec(memory_space=pltpu.VMEM)] * len(fields),
+        out_specs=pl.BlockSpec(memory_space=pltpu.VMEM),
+        cost_estimate=pl.CostEstimate(
+            flops=0,
+            transcendentals=0,
+            bytes_accessed=4 * len(fields) * rows * width,
+        ),
+    )(*fields)
+
+
 def unshuffle_kernel(first_ref, rest_ref, *out_refs):
     head_count, _, head_dim = first_ref.shape
     for i, out_ref in enumerate(out_refs):
@@ -171,15 +197,9 @@
 
 
 def local(queries, key_states, value_states, upstream, layout, segments):
-    section_rows, tok_dev, feature_width = queries.shape
-    head_dim = feature_width // HEADS
-
-    def head_major(field):
-        return field.reshape(tok_dev, HEADS, head_dim).transpose(1, 0, 2)
-
-    fields = jnp.stack(
-        [head_major(f) for f in (queries, key_states, value_states, upstream)], axis=1
-    )
+    section_rows, _, _ = queries.shape
+
+    fields = shuffle((queries, key_states, value_states, upstream), HEADS)
     fields = lax.all_to_all(fields, "ctx", 0, 0, tiled=True)
     block_count = fields.shape[0]
     plan = layout[0, 0].reshape(block_count * SLOTS)

time: 172 us -> 163 us (0.948)
  local copies, waits for them, and re-layouts: 11.2 us -> 3.88 us
    unnamed x17 -> x9, local copies, waits for them, and re-layouts: 6.92 us -> 2.2 us
    pallas_call x0 -> x1, Pallas kernels: none -> 3.22 us  [shuffle(): pl.pallas_call(shuffle_kernel, out_shape=out, in_specs=[pl.BlockSpec(memo...]
    another operation x1 -> x0, local copies, waits for them, and re-layouts: 2.61 us -> none  [local(): jnp.stack([head_major(f) for f in (queries, key_states, value_states, ups...]
    pallas_call x1, Pallas kernels: 11.6 us -> 9.75 us  [backward_pass(): pl.pallas_call(backward_kernel, out_shape=jax.ShapeDtypeStruct((block_cou...]
    pallas_call x1, Pallas kernels: 11.7 us -> 9.9 us  [forward_pass(): pl.pallas_call(forward_kernel, out_shape=[jax.ShapeDtypeStruct((block_cou...]
  transfers between devices with their start and end apart: 3 -> 3, of which waited for: 2 -> 2; matrix products, arithmetic and copies ran while one was open for 1% -> 1% of each run, Pallas kernels for 7% -> 6%
where the time goes in v2:
time: 163 us; the launch traced here: 162 us
  waiting for transfers between devices  59.5 us (37%)
  blocking collectives  47.6 us (29%)
  Pallas kernels  26.3 us (16%)
  starting transfers between devices  24.1 us (15%)
  local copies, waits for them, and re-layouts  3.88 us (2%)
    all_to_all x1, waiting for transfers between devices, local(): fields = lax.all_to_all(fields, 'ctx', 0, 0, tiled=True)  48.4 us
    all_to_all x1, blocking collectives, local(): back = lax.all_to_all(results, 'ctx', 0, 0, tiled=True)  47.6 us
    all_to_all x1, starting transfers between devices, local(): fields = lax.all_to_all(fields, 'ctx', 0, 0, tiled=True)  12 us
    ppermute x1, waiting for transfers between devices, passed_along(): return lax.ppermute(value, axis, pairs)  11.2 us
    pallas_call x1, Pallas kernels, forward_pass(): pl.pallas_call(forward_kernel, out_shape=[jax.ShapeDtypeStruct((block_cou...  9.9 us
    pallas_call x1, Pallas kernels, backward_pass(): pl.pallas_call(backward_kernel, out_shape=jax.ShapeDtypeStruct((block_cou...  9.75 us
    ppermute x1, starting transfers between devices, passed_along(): return lax.ppermute(value, axis, pairs)  7.29 us
    all_to_all x1, starting transfers between devices, local(): attended_back = lax.all_to_all(attended, 'ctx', 0, 0, tiled=True)  4.84 us
  transfers between devices with their start and end apart: 3, of which 2 were waited for; matrix products, arithmetic and copies ran while one was open for 1% of the time, Pallas kernels for 6%

profile of v2, /device:TPU:1, one launch (start us, length us, event | category | flops | bytes accessed | tf_op | source)
XLA Modules:
  0.0 162.0 jit_solution(5495637011463889009)
XLA Ops:
  0.6 3.2 %shard_map.93 = bf16[16,4,128,128]{3,2,1,0:T(8,128)(2,1)} custom-call(bf16[1,128,2048]{2,1,0:T(8,128)(2,1)} %refs_0_.1, bf16[1,128,2048]{2,1,0:T(8,128)(2,1)} %refs_1_.1, bf16[1,128,2048]{2,1,0:T(8,128)(2,1)} %refs_2_.1, bf16[1,128,2048]{2,1,0:T(8,128)(2,1)} %refs_3_.1), custom_call_target="tpu_custom_call" | custom-call | bytes 4194304 | tf_op jit(solution)/shard_map/pallas_call | solution.py:162
  3.8 0.0 copy-start.3
  3.9 12.0 %all-to-all-start = ((bf16[16,4,128,128]{3,2,1,0:T(8,128)(2,1)}), bf16[16,4,128,128]{3,2,1,0:T(8,128)(2,1)S(1)}, u32[]{:S(2)}, u32[]{:S(2)}) async-start(bf16[16,4,128,128]{3,2,1,0:T(8,128)(2,1)} %shard_map.93), calls=%async_computation | async-start | bytes 4194304 | tf_op jit(solution)/shard_map/all_to_all | solution.py:203
  15.8 0.0 copy-done.3
  15.8 0.1 copy.18
  15.9 0.6 reshape_squeeze.3.lay_ref
  16.5 48.4 %all-to-all-done.qkv_ref = bf16[16,4,128,128]{3,2,1,0:T(8,128)(2,1)S(1)} async-done(((bf16[16,4,128,128]{3,2,1,0:T(8,128)(2,1)}), bf16[16,4,128,128]{3,2,1,0:T(8,128)(2,1)S(1)}, u32[]{:S(2)}, u32[]{:S(2)}) %all-to-all-start) | async-done | bytes 2097184 | tf_op jit(solution)/shard_map/all_to_all | solution.py:203
  64.9 0.0 copy-start
  64.9 1.3 copy-done
  66.2 9.9 %shard_map.94 = (bf16[16,128,128]{2,1,0:T(8,128)(2,1)}, f32[16,128,512]{2,1,0:T(8,128)}) custom-call(s32[64]{0:T(128)} %reshape_squeeze.3.lay_ref, s32[16]{0:T(128)} %bitcast.7, bf16[16,4,128,128]{3,2,1,0:T(8,128)(2,1)} %copy-done), custom_call_target="tpu_custom_call" | custom-call | flops 536870912 | bytes 6291456 | tf_op jit(solution)/shard_map/pallas_call | solution.py:106
  76.1 4.8 %all-to-all-start.1 = ((bf16[16,128,128]{2,1,0:T(8,128)(2,1)}), bf16[16,128,128]{2,1,0:T(8,128)(2,1)S(1)}, u32[]{:S(2)}, u32[]{:S(2)}) async-start(bf16[16,128,128]{2,1,0:T(8,128)(2,1)} %get-tuple-element.6.o_ref), calls=%async_computation.1 | async-start | bytes 1048576 | tf_op jit(solution)/shard_map/all_to_all | solution.py:209
  80.9 1.1 slice_bitcast_fusion
  82.0 7.3 %collective-permute-start = (bf16[16,128,128]{2,1,0:T(8,128)(2,1)S(1)}, bf16[16,128,128]{2,1,0:T(8,128)(2,1)S(1)}, u32[]{:S(2)}, u32[]{:S(2)}) collective-permute-start(bf16[16,128,128]{2,1,0:T(8,128)(2,1)S(1)} %slice_bitcast_fusion), channel_id=1, source_target_pairs={{0,496},{16,0},{32,16},{48,32},{64,48},{80,64},{96,80},{112,96},{1... | collective-permute-start | bytes 1572872 | tf_op jit(solution)/shard_map/ppermute | solution.py:19
  89.3 11.2 %collective-permute-done.g_ref = bf16[16,128,128]{2,1,0:T(8,128)(2,1)S(1)} collective-permute-done((bf16[16,128,128]{2,1,0:T(8,128)(2,1)S(1)}, bf16[16,128,128]{2,1,0:T(8,128)(2,1)S(1)}, u32[]{:S(2)}, u32[]{:S(2)}) %collective-permute-start) | collective-permute-done | bytes 524320 | tf_op jit(solution)/shard_map/ppermute | solution.py:19
  100.4 0.0 copy-start.2
  100.4 0.8 copy-done.2
  101.2 9.7 %shard_map.95 = bf16[16,3,128,128]{3,2,1,0:T(8,128)(2,1)} custom-call(s32[64]{0:T(128)} %reshape_squeeze.3.lay_ref, bf16[16,4,128,128]{3,2,1,0:T(8,128)(2,1)} %copy-done, bf16[16,128,128]{2,1,0:T(8,128)(2,1)} %copy-done.2, bf16[16,128,128]{2,1,0:T(8,128)(2,1)} %get-tuple-element.6.o_ref, f32[16,128,512]{2,1,0:T(8,128)} %get-tuple-element.7.w_ref), custom_call_target="tpu_custom_call" | custom-call | flops 1073741824 | bytes 8912896 | tf_op jit(solution)/shard_map/pallas_call | solution.py:130
  111.0 0.0 all-to-all-done.1.first_ref
  111.0 0.0 copy-start.1
  111.0 47.6 %all_to_all.15.rest_ref = bf16[16,3,128,128]{3,2,1,0:T(8,128)(2,1)} all-to-all(bf16[16,3,128,128]{3,2,1,0:T(8,128)(2,1)} %shard_map.95), channel_id=1, replica_groups=mesh['section'=32,'ctx'=16] {'ctx'}, dimensions={0} | all-to-all | bytes 3145728 | tf_op jit(solution)/shard_map/all_to_all | solution.py:211
  158.6 0.0 copy-done.1
  158.6 3.4 %shard_map.96 = (bf16[1,128,2048]{2,1,0:T(8,128)(2,1)}, bf16[1,128,2048]{2,1,0:T(8,128)(2,1)}, bf16[1,128,2048]{2,1,0:T(8,128)(2,1)}, bf16[1,128,2048]{2,1,0:T(8,128)(2,1)}) custom-call(bf16[16,128,128]{2,1,0:T(8,128)(2,1)} %copy-done.1, bf16[16,3,128,128]{3,2,1,0:T(8,128)(2,1)} %all_to_all.15.rest_ref), custom_call_target="tpu_custom_call" | custom-call | bytes 4194304 | tf_op jit(solution)/shard_map/pallas_call | solution.py:186
Async XLA Ops:
  3.8 12.0 %copy-start.3 = (s32[1,1,16,4]{2,3,1,0:T(4,128)S(1)}, s32[1,1,16,4]{2,3,1,0:T(4,128)}, u32[]{:S(2)}) copy-start(s32[1,1,16,4]{2,3,1,0:T(4,128)} %param.10) | copy-start | bytes 772
  3.9 61.0 %all-to-all-start = ((bf16[16,4,128,128]{3,2,1,0:T(8,128)(2,1)}), bf16[16,4,128,128]{3,2,1,0:T(8,128)(2,1)S(1)}, u32[]{:S(2)}, u32[]{:S(2)}) async-start(bf16[16,4,128,128]{3,2,1,0:T(8,128)(2,1)} %shard_map.93), calls=%async_computation | async-start | bytes 4194304 | tf_op jit(solution)/shard_map/all_to_all | solution.py:203
  64.9 1.3 copy-start
  76.1 34.9 %all-to-all-start.1 = ((bf16[16,128,128]{2,1,0:T(8,128)(2,1)}), bf16[16,128,128]{2,1,0:T(8,128)(2,1)S(1)}, u32[]{:S(2)}, u32[]{:S(2)}) async-start(bf16[16,128,128]{2,1,0:T(8,128)(2,1)} %get-tuple-element.6.o_ref), calls=%async_computation.1 | async-start | bytes 1048576 | tf_op jit(solution)/shard_map/all_to_all | solution.py:209
  82.0 18.4 %collective-permute-start = (bf16[16,128,128]{2,1,0:T(8,128)(2,1)S(1)}, bf16[16,128,128]{2,1,0:T(8,128)(2,1)S(1)}, u32[]{:S(2)}, u32[]{:S(2)}) collective-permute-start(bf16[16,128,128]{2,1,0:T(8,128)(2,1)S(1)} %slice_bitcast_fusion), channel_id=1, source_target_pairs={{0,496},{16,0},{32,16},{48,32},{64,48},{80,64},{96,80},{112,96},{1... | collective-permute-start | bytes 1572872 | tf_op jit(solution)/shard_map/ppermute | solution.py:19
  100.4 0.8 copy-start.2
  111.0 47.6 %copy-start.1 = (bf16[16,128,128]{2,1,0:T(8,128)(2,1)}, bf16[16,128,128]{2,1,0:T(8,128)(2,1)S(1)}, u32[]{:S(2)}) copy-start(bf16[16,128,128]{2,1,0:T(8,128)(2,1)S(1)} %all-to-all-done.1.first_ref) | copy-start | bytes 1572868

commit v3 on v2

--- a/solution.py
+++ b/solution.py
@@ -197,14 +197,15 @@
 
 
 def local(queries, key_states, value_states, upstream, layout, segments):
-    section_rows, _, _ = queries.shape
-
-    fields = shuffle((queries, key_states, value_states, upstream), HEADS)
+    section_rows = queries.shape[0]
+    fields = shuffle((queries, key_states, value_states), HEADS)
     fields = lax.all_to_all(fields, "ctx", 0, 0, tiled=True)
+    arrived = passed_along(upstream, "section", -1)
+    grad = shuffle((arrived,), HEADS)
+    grad = lax.all_to_all(grad, "ctx", 0, 0, tiled=True)[:, 0]
     block_count = fields.shape[0]
     plan = layout[0, 0].reshape(block_count * SLOTS)
     documents = segments[0]
-    grad = passed_along(fields[:, 3], "section", -1)
     attended, weights = forward_pass(plan, documents, fields)
     attended_back = lax.all_to_all(attended, "ctx", 0, 0, tiled=True)
     results = backward_pass(plan, fields, grad, attended, weights)

time: 163 us -> 142 us (0.87)
  waiting for transfers between devices: 59.5 us -> 42.3 us
  blocking collectives: 47.6 us -> 43 us
  starting transfers between devices: 24.1 us -> 26.9 us
  local copies, waits for them, and re-layouts: 3.88 us -> 1.5 us
    all_to_all x1, waiting for transfers between devices: 48.4 us -> 17.3 us  [local(): fields = lax.all_to_all(fields, 'ctx', 0, 0, tiled=True)]
    all_to_all x1, waiting for transfers between devices: 0.01 us -> 7.06 us  [local(): attended_back = lax.all_to_all(attended, 'ctx', 0, 0, tiled=True)]
    all_to_all x0 -> x1, waiting for transfers between devices: none -> 6.8 us  [local(): grad = lax.all_to_all(grad, 'ctx', 0, 0, tiled=True)[:, 0]]
    all_to_all x1, blocking collectives: 47.6 us -> 43 us  [local(): back = lax.all_to_all(results, 'ctx', 0, 0, tiled=True)]
    all_to_all x0 -> x1, starting transfers between devices: none -> 4.14 us  [local(): grad = lax.all_to_all(grad, 'ctx', 0, 0, tiled=True)[:, 0]]
    pallas_call x1 -> x2, Pallas kernels: 3.22 us -> 4.72 us  [shuffle(): pl.pallas_call(shuffle_kernel, out_shape=out, in_specs=[pl.BlockSpec(memo...]
  transfers between devices with their start and end apart: 3 -> 4, of which waited for: 2 -> 4; matrix products, arithmetic and copies ran while one was open for 1% -> 0% of each run, Pallas kernels for 6% -> 15%
where the time goes in v3:
time: 142 us
  blocking collectives  43 us (30%)
  waiting for transfers between devices  42.3 us (30%)
  Pallas kernels  27.5 us (19%)
  starting transfers between devices  26.9 us (19%)
  local copies, waits for them, and re-layouts  1.5 us (1%)
    all_to_all x1, blocking collectives, local(): back = lax.all_to_all(results, 'ctx', 0, 0, tiled=True)  43 us
    all_to_all x1, waiting for transfers between devices, local(): fields = lax.all_to_all(fields, 'ctx', 0, 0, tiled=True)  17.3 us
    all_to_all x1, starting transfers between devices, local(): fields = lax.all_to_all(fields, 'ctx', 0, 0, tiled=True)  12 us
    ppermute x1, waiting for transfers between devices, passed_along(): return lax.ppermute(value, axis, pairs)  11.2 us
    pallas_call x1, Pallas kernels, forward_pass(): pl.pallas_call(forward_kernel, out_shape=[jax.ShapeDtypeStruct((block_cou...  9.71 us
    pallas_call x1, Pallas kernels, backward_pass(): pl.pallas_call(backward_kernel, out_shape=jax.ShapeDtypeStruct((block_cou...  9.62 us
    ppermute x1, starting transfers between devices, passed_along(): return lax.ppermute(value, axis, pairs)  7.29 us
    all_to_all x1, waiting for transfers between devices, local(): attended_back = lax.all_to_all(attended, 'ctx', 0, 0, tiled=True)  7.06 us
  transfers between devices with their start and end apart: 4, of which 4 were waited for; matrix products, arithmetic and copies ran while one was open for 0% of the time, Pallas kernels for 15%

profile of v3, /device:TPU:1, one launch (start us, length us, event | category | flops | bytes accessed | tf_op | source)
XLA Modules:
  0.0 141.8 jit_solution(8831265671652585851)
XLA Ops:
  0.6 2.8 %shard_map.93 = bf16[16,3,128,128]{3,2,1,0:T(8,128)(2,1)} custom-call(bf16[1,128,2048]{2,1,0:T(8,128)(2,1)} %refs_0_.1, bf16[1,128,2048]{2,1,0:T(8,128)(2,1)} %refs_1_.1, bf16[1,128,2048]{2,1,0:T(8,128)(2,1)} %refs_2_.1), custom_call_target="tpu_custom_call" | custom-call | bytes 3145728 | tf_op jit(solution)/shard_map/pallas_call | solution.py:162
  3.4 0.0 copy-start.5
  3.4 12.0 %all-to-all-start = ((bf16[16,3,128,128]{3,2,1,0:T(8,128)(2,1)}), bf16[16,3,128,128]{3,2,1,0:T(8,128)(2,1)S(1)}, u32[]{:S(2)}, u32[]{:S(2)}) async-start(bf16[16,3,128,128]{3,2,1,0:T(8,128)(2,1)} %shard_map.93), calls=%async_computation | async-start | bytes 3145728 | tf_op jit(solution)/shard_map/all_to_all | solution.py:202
  15.4 0.0 copy-done.5
  15.4 0.0 copy-start.4
  15.4 7.3 %collective-permute-start = (bf16[1,128,2048]{2,1,0:T(8,128)(2,1)S(1)}, bf16[1,128,2048]{2,1,0:T(8,128)(2,1)S(1)}, u32[]{:S(2)}, u32[]{:S(2)}) collective-permute-start(bf16[1,128,2048]{2,1,0:T(8,128)(2,1)S(1)} %copy-done.5), channel_id=1, source_target_pairs={{0,496},{16,0},{32,16},{48,32},{64,48},{80,64},{96,80},{112,96},{1... | collective-permute-start | bytes 1572872 | tf_op jit(solution)/shard_map/ppermute | solution.py:19
  22.7 11.2 %collective-permute-done.refs_0_ = bf16[1,128,2048]{2,1,0:T(8,128)(2,1)S(1)} collective-permute-done((bf16[1,128,2048]{2,1,0:T(8,128)(2,1)S(1)}, bf16[1,128,2048]{2,1,0:T(8,128)(2,1)S(1)}, u32[]{:S(2)}, u32[]{:S(2)}) %collective-permute-start) | collective-permute-done | bytes 524320 | tf_op jit(solution)/shard_map/ppermute | solution.py:19
  33.9 0.8 copy-done.3
  34.6 1.9 %shard_map.95 = bf16[16,1,128,128]{3,2,1,0:T(8,128)(2,1)} custom-call(bf16[1,128,2048]{2,1,0:T(8,128)(2,1)} %copy-done.3), custom_call_target="tpu_custom_call" | custom-call | bytes 1048576 | tf_op jit(solution)/shard_map/pallas_call | solution.py:162
  36.6 17.3 %all-to-all-done.qkv_ref = bf16[16,3,128,128]{3,2,1,0:T(8,128)(2,1)S(1)} async-done(((bf16[16,3,128,128]{3,2,1,0:T(8,128)(2,1)}), bf16[16,3,128,128]{3,2,1,0:T(8,128)(2,1)S(1)}, u32[]{:S(2)}, u32[]{:S(2)}) %all-to-all-start) | async-done | bytes 1572896 | tf_op jit(solution)/shard_map/all_to_all | solution.py:202
  53.9 4.1 %all-to-all-start.2 = ((bf16[16,1,128,128]{3,2,1,0:T(8,128)(2,1)}), bf16[16,1,128,128]{3,2,1,0:T(8,128)(2,1)S(1)}, u32[]{:S(2)}, u32[]{:S(2)}) async-start(bf16[16,1,128,128]{3,2,1,0:T(8,128)(2,1)} %shard_map.95), calls=%async_computation.2 | async-start | bytes 1048576 | tf_op jit(solution)/shard_map/all_to_all | solution.py:205
  58.0 0.0 copy-done.4
  58.0 0.1 copy.14
  58.1 0.6 reshape_squeeze.3.lay_ref
  58.7 0.0 copy-done
  58.7 9.7 %shard_map.94 = (bf16[16,128,128]{2,1,0:T(8,128)(2,1)}, f32[16,128,512]{2,1,0:T(8,128)}) custom-call(s32[64]{0:T(128)} %reshape_squeeze.3.lay_ref, s32[16]{0:T(128)} %bitcast.5, bf16[16,3,128,128]{3,2,1,0:T(8,128)(2,1)} %copy-done), custom_call_target="tpu_custom_call" | custom-call | flops 536870912 | bytes 6291456 | tf_op jit(solution)/shard_map/pallas_call | solution.py:106
  68.4 6.8 %all-to-all-done.2 = bf16[16,1,128,128]{3,2,1,0:T(8,128)(2,1)S(1)} async-done(((bf16[16,1,128,128]{3,2,1,0:T(8,128)(2,1)}), bf16[16,1,128,128]{3,2,1,0:T(8,128)(2,1)S(1)}, u32[]{:S(2)}, u32[]{:S(2)}) %all-to-all-start.2) | async-done | bytes 524320 | tf_op jit(solution)/shard_map/all_to_all | solution.py:205
  75.2 3.5 %all-to-all-start.1 = ((bf16[16,128,128]{2,1,0:T(8,128)(2,1)}), bf16[16,128,128]{2,1,0:T(8,128)(2,1)S(1)}, u32[]{:S(2)}, u32[]{:S(2)}) async-start(bf16[16,128,128]{2,1,0:T(8,128)(2,1)} %get-tuple-element.6.o_ref), calls=%async_computation.1 | async-start | bytes 1048576 | tf_op jit(solution)/shard_map/all_to_all | solution.py:210
  78.7 0.0 copy-done.1
  78.7 9.6 %shard_map.96 = bf16[16,3,128,128]{3,2,1,0:T(8,128)(2,1)} custom-call(s32[64]{0:T(128)} %reshape_squeeze.3.lay_ref, bf16[16,3,128,128]{3,2,1,0:T(8,128)(2,1)} %copy-done, bf16[16,128,128]{2,1,0:T(8,128)(2,1)} %bitcast.4, bf16[16,128,128]{2,1,0:T(8,128)(2,1)} %get-tuple-element.6.o_ref, f32[16,128,512]{2,1,0:T(8,128)} %get-tuple-element.7.w_ref), custom_call_target="tpu_custom_call" | custom-call | flops 1073741824 | bytes 8912896 | tf_op jit(solution)/shard_map/pallas_call | solution.py:130
  88.4 7.1 %all-to-all-done.1.first_ref = bf16[16,128,128]{2,1,0:T(8,128)(2,1)S(1)} async-done(((bf16[16,128,128]{2,1,0:T(8,128)(2,1)}), bf16[16,128,128]{2,1,0:T(8,128)(2,1)S(1)}, u32[]{:S(2)}, u32[]{:S(2)}) %all-to-all-start.1) | async-done | bytes 524320 | tf_op jit(solution)/shard_map/all_to_all | solution.py:210
  95.4 43.0 %all_to_all.20.rest_ref = bf16[16,3,128,128]{3,2,1,0:T(8,128)(2,1)} all-to-all(bf16[16,3,128,128]{3,2,1,0:T(8,128)(2,1)} %shard_map.96), channel_id=1, replica_groups=mesh['section'=32,'ctx'=16] {'ctx'}, dimensions={0} | all-to-all | bytes 3145728 | tf_op jit(solution)/shard_map/all_to_all | solution.py:212
  138.4 0.0 copy-done.2
  138.4 3.4 %shard_map.97 = (bf16[1,128,2048]{2,1,0:T(8,128)(2,1)}, bf16[1,128,2048]{2,1,0:T(8,128)(2,1)}, bf16[1,128,2048]{2,1,0:T(8,128)(2,1)}, bf16[1,128,2048]{2,1,0:T(8,128)(2,1)}) custom-call(bf16[16,128,128]{2,1,0:T(8,128)(2,1)} %copy-done.2, bf16[16,3,128,128]{3,2,1,0:T(8,128)(2,1)} %all_to_all.20.rest_ref), custom_call_target="tpu_custom_call" | custom-call | bytes 4194304 | tf_op jit(solution)/shard_map/pallas_call | solution.py:186
  (4 shorter events, 0.0 us)
Async XLA Ops:
  3.4 12.0 %copy-start.5 = (bf16[1,128,2048]{2,1,0:T(8,128)(2,1)S(1)}, bf16[1,128,2048]{2,1,0:T(8,128)(2,1)}, u32[]{:S(2)}) copy-start(bf16[1,128,2048]{2,1,0:T(8,128)(2,1)} %param.9) | copy-start | bytes 1572868
  3.4 50.5 %all-to-all-start = ((bf16[16,3,128,128]{3,2,1,0:T(8,128)(2,1)}), bf16[16,3,128,128]{3,2,1,0:T(8,128)(2,1)S(1)}, u32[]{:S(2)}, u32[]{:S(2)}) async-start(bf16[16,3,128,128]{3,2,1,0:T(8,128)(2,1)} %shard_map.93), calls=%async_computation | async-start | bytes 3145728 | tf_op jit(solution)/shard_map/all_to_all | solution.py:202
  15.4 42.7 %copy-start.4 = (s32[1,1,16,4]{2,3,1,0:T(4,128)S(1)}, s32[1,1,16,4]{2,3,1,0:T(4,128)}, u32[]{:S(2)}) copy-start(s32[1,1,16,4]{2,3,1,0:T(4,128)} %param.10) | copy-start | bytes 772
  15.4 18.5 %collective-permute-start = (bf16[1,128,2048]{2,1,0:T(8,128)(2,1)S(1)}, bf16[1,128,2048]{2,1,0:T(8,128)(2,1)S(1)}, u32[]{:S(2)}, u32[]{:S(2)}) collective-permute-start(bf16[1,128,2048]{2,1,0:T(8,128)(2,1)S(1)} %copy-done.5), channel_id=1, source_target_pairs={{0,496},{16,0},{32,16},{48,32},{64,48},{80,64},{96,80},{112,96},{1... | collective-permute-start | bytes 1572872 | tf_op jit(solution)/shard_map/ppermute | solution.py:19
  33.9 0.8 copy-start.3
  53.9 4.8 %copy-start = (bf16[16,3,128,128]{3,2,1,0:T(8,128)(2,1)}, bf16[16,3,128,128]{3,2,1,0:T(8,128)(2,1)S(1)}, u32[]{:S(2)}) copy-start(bf16[16,3,128,128]{3,2,1,0:T(8,128)(2,1)S(1)} %all-to-all-done.qkv_ref) | copy-start | bytes 4718596
  53.9 21.3 %all-to-all-start.2 = ((bf16[16,1,128,128]{3,2,1,0:T(8,128)(2,1)}), bf16[16,1,128,128]{3,2,1,0:T(8,128)(2,1)S(1)}, u32[]{:S(2)}, u32[]{:S(2)}) async-start(bf16[16,1,128,128]{3,2,1,0:T(8,128)(2,1)} %shard_map.95), calls=%async_computation.2 | async-start | bytes 1048576 | tf_op jit(solution)/shard_map/all_to_all | solution.py:205
  75.2 3.5 %copy-start.1 = (bf16[16,1,128,128]{3,2,1,0:T(8,128)(2,1)}, bf16[16,1,128,128]{3,2,1,0:T(8,128)(2,1)S(1)}, u32[]{:S(2)}) copy-start(bf16[16,1,128,128]{3,2,1,0:T(8,128)(2,1)S(1)} %all-to-all-done.2) | copy-start | bytes 1572868
  75.2 20.2 %all-to-all-start.1 = ((bf16[16,128,128]{2,1,0:T(8,128)(2,1)}), bf16[16,128,128]{2,1,0:T(8,128)(2,1)S(1)}, u32[]{:S(2)}, u32[]{:S(2)}) async-start(bf16[16,128,128]{2,1,0:T(8,128)(2,1)} %get-tuple-element.6.o_ref), calls=%async_computation.1 | async-start | bytes 1048576 | tf_op jit(solution)/shard_map/all_to_all | solution.py:210
  95.4 43.0 %copy-start.2 = (bf16[16,128,128]{2,1,0:T(8,128)(2,1)}, bf16[16,128,128]{2,1,0:T(8,128)(2,1)S(1)}, u32[]{:S(2)}) copy-start(bf16[16,128,128]{2,1,0:T(8,128)(2,1)S(1)} %all-to-all-done.1.first_ref) | copy-start | bytes 1572868

commit v4 on v3

--- a/solution.py
+++ b/solution.py
@@ -172,28 +172,26 @@
     )(*fields)
 
 
-def unshuffle_kernel(first_ref, rest_ref, *out_refs):
-    head_count, _, head_dim = first_ref.shape
+def unshuffle_kernel(back_ref, *out_refs):
+    head_count = back_ref.shape[0]
+    head_dim = back_ref.shape[-1]
     for i, out_ref in enumerate(out_refs):
         for h in range(head_count):
-            piece = first_ref[h] if i == 0 else rest_ref[h, i - 1]
-            out_ref[0, :, h * head_dim:(h + 1) * head_dim] = piece
-
-
-def unshuffle(first, rest, section_rows):
-    head_count, arrays, rows, head_dim = rest.shape
-    field = jax.ShapeDtypeStruct((section_rows, rows, head_count * head_dim), rest.dtype)
+            out_ref[0, :, h * head_dim:(h + 1) * head_dim] = back_ref[h, i]
+
+
+def unshuffle(back, section_rows):
+    head_count, arrays, rows, head_dim = back.shape
+    field = jax.ShapeDtypeStruct((section_rows, rows, head_count * head_dim), back.dtype)
     return pl.pallas_call(
         unshuffle_kernel,
-        out_shape=[field] * (arrays + 1),
-        in_specs=[pl.BlockSpec(memory_space=pltpu.VMEM)] * 2,
-        out_specs=[pl.BlockSpec(memory_space=pltpu.VMEM)] * (arrays + 1),
-        cost_estimate=pl.CostEstimate(
-            flops=0,
-            transcendentals=0,
-            bytes_accessed=4 * (first.size + rest.size),
-        ),
-    )(first, rest)
+        out_shape=[field] * arrays,
+        in_specs=[pl.BlockSpec(memory_space=pltpu.VMEM)],
+        out_specs=[pl.BlockSpec(memory_space=pltpu.VMEM)] * arrays,
+        cost_estimate=pl.CostEstimate(
+            flops=0, transcendentals=0, bytes_accessed=4 * back.size
+        ),
+    )(back)
 
 
 def local(queries, key_states, value_states, upstream, layout, segments):
@@ -210,7 +208,8 @@
     attended_back = lax.all_to_all(attended, "ctx", 0, 0, tiled=True)
     results = backward_pass(plan, fields, grad, attended, weights)
     back = lax.all_to_all(results, "ctx", 0, 0, tiled=True)
-    return tuple(unshuffle(attended_back, back, section_rows))
+    (attended_out,) = unshuffle(attended_back[:, None], section_rows)
+    return (attended_out, *unshuffle(back, section_rows))
 
 
 def solution(mesh):

time: 142 us -> 142 us (level)
  blocking collectives: 43 us -> 0 us
  waiting for transfers between devices: 42.3 us -> 78.2 us
  starting transfers between devices: 26.9 us -> 30.5 us
  local copies, waits for them, and re-layouts: 1.5 us -> 3.46 us
  Pallas kernels: 27.5 us -> 29 us
    all_to_all x1 -> x0, blocking collectives: 43 us -> none  [local(): back = lax.all_to_all(results, 'ctx', 0, 0, tiled=True)]
    all_to_all x0 -> x1, waiting for transfers between devices: none -> 35.9 us  [local(): back = lax.all_to_all(results, 'ctx', 0, 0, tiled=True)]
    all_to_all x0 -> x1, starting transfers between devices: none -> 3.6 us  [local(): back = lax.all_to_all(results, 'ctx', 0, 0, tiled=True)]
    unnamed x13 -> x15, local copies, waits for them, and re-layouts: 0.9 us -> 2.86 us
    pallas_call x1 -> x2, Pallas kernels: 3.43 us -> 4.92 us  [unshuffle(): pl.pallas_call(unshuffle_kernel, out_shape=[field] * arrays, in_specs=[pl...]
  transfers between devices with their start and end apart: 4 -> 5, of which waited for: 4 -> 5; matrix products, arithmetic and copies ran while one was open for 0% -> 0% of each run, Pallas kernels for 15% -> 16%
where the time goes in v4:
time: 142 us
  waiting for transfers between devices  78.2 us (55%)
  starting transfers between devices  30.5 us (21%)
  Pallas kernels  29 us (20%)
  local copies, waits for them, and re-layouts  3.46 us (2%)
    all_to_all x1, waiting for transfers between devices, local(): back = lax.all_to_all(results, 'ctx', 0, 0, tiled=True)  35.9 us
    all_to_all x1, waiting for transfers between devices, local(): fields = lax.all_to_all(fields, 'ctx', 0, 0, tiled=True)  17.3 us
    all_to_all x1, starting transfers between devices, local(): fields = lax.all_to_all(fields, 'ctx', 0, 0, tiled=True)  12 us
    ppermute x1, waiting for transfers between devices, passed_along(): return lax.ppermute(value, axis, pairs)  11.2 us
    pallas_call x1, Pallas kernels, forward_pass(): pl.pallas_call(forward_kernel, out_shape=[jax.ShapeDtypeStruct((block_cou...  9.72 us
    pallas_call x1, Pallas kernels, backward_pass(): pl.pallas_call(backward_kernel, out_shape=jax.ShapeDtypeStruct((block_cou...  9.65 us
    ppermute x1, starting transfers between devices, passed_along(): return lax.ppermute(value, axis, pairs)  7.29 us
    all_to_all x1, waiting for transfers between devices, local(): attended_back = lax.all_to_all(attended, 'ctx', 0, 0, tiled=True)  7.03 us
  transfers between devices with their start and end apart: 5, of which 5 were waited for; matrix products, arithmetic and copies ran while one was open for 0% of the time, Pallas kernels for 16%

profile of v4, /device:TPU:1, one launch (start us, length us, event | category | flops | bytes accessed | tf_op | source)
XLA Modules:
  0.0 141.8 jit_solution(387791739757223435)
XLA Ops:
  0.6 2.8 %shard_map.93 = bf16[16,3,128,128]{3,2,1,0:T(8,128)(2,1)} custom-call(bf16[1,128,2048]{2,1,0:T(8,128)(2,1)} %refs_0_.1, bf16[1,128,2048]{2,1,0:T(8,128)(2,1)} %refs_1_.1, bf16[1,128,2048]{2,1,0:T(8,128)(2,1)} %refs_2_.1), custom_call_target="tpu_custom_call" | custom-call | bytes 3145728 | tf_op jit(solution)/shard_map/pallas_call | solution.py:162
  3.4 12.0 %all-to-all-start = ((bf16[16,3,128,128]{3,2,1,0:T(8,128)(2,1)}), bf16[16,3,128,128]{3,2,1,0:T(8,128)(2,1)S(1)}, u32[]{:S(2)}, u32[]{:S(2)}) async-start(bf16[16,3,128,128]{3,2,1,0:T(8,128)(2,1)} %shard_map.93), calls=%async_computation | async-start | bytes 3145728 | tf_op jit(solution)/shard_map/all_to_all | solution.py:200
  15.4 0.0 copy-done.6
  15.4 0.0 copy-start.5
  15.4 7.3 %collective-permute-start = (bf16[1,128,2048]{2,1,0:T(8,128)(2,1)S(1)}, bf16[1,128,2048]{2,1,0:T(8,128)(2,1)S(1)}, u32[]{:S(2)}, u32[]{:S(2)}) collective-permute-start(bf16[1,128,2048]{2,1,0:T(8,128)(2,1)S(1)} %copy-done.6), channel_id=1, source_target_pairs={{0,496},{16,0},{32,16},{48,32},{64,48},{80,64},{96,80},{112,96},{1... | collective-permute-start | bytes 1572872 | tf_op jit(solution)/shard_map/ppermute | solution.py:19
  22.7 11.2 %collective-permute-done.refs_0_ = bf16[1,128,2048]{2,1,0:T(8,128)(2,1)S(1)} collective-permute-done((bf16[1,128,2048]{2,1,0:T(8,128)(2,1)S(1)}, bf16[1,128,2048]{2,1,0:T(8,128)(2,1)S(1)}, u32[]{:S(2)}, u32[]{:S(2)}) %collective-permute-start) | collective-permute-done | bytes 524320 | tf_op jit(solution)/shard_map/ppermute | solution.py:19
  33.9 0.8 copy-done.4
  34.7 1.9 %shard_map.96 = bf16[16,1,128,128]{3,2,1,0:T(8,128)(2,1)} custom-call(bf16[1,128,2048]{2,1,0:T(8,128)(2,1)} %copy-done.4), custom_call_target="tpu_custom_call" | custom-call | bytes 1048576 | tf_op jit(solution)/shard_map/pallas_call | solution.py:162
  36.6 17.3 %all-to-all-done.qkv_ref = bf16[16,3,128,128]{3,2,1,0:T(8,128)(2,1)S(1)} async-done(((bf16[16,3,128,128]{3,2,1,0:T(8,128)(2,1)}), bf16[16,3,128,128]{3,2,1,0:T(8,128)(2,1)S(1)}, u32[]{:S(2)}, u32[]{:S(2)}) %all-to-all-start) | async-done | bytes 1572896 | tf_op jit(solution)/shard_map/all_to_all | solution.py:200
  53.9 4.1 %all-to-all-start.2 = ((bf16[16,1,128,128]{3,2,1,0:T(8,128)(2,1)}), bf16[16,1,128,128]{3,2,1,0:T(8,128)(2,1)S(1)}, u32[]{:S(2)}, u32[]{:S(2)}) async-start(bf16[16,1,128,128]{3,2,1,0:T(8,128)(2,1)} %shard_map.96), calls=%async_computation.2 | async-start | bytes 1048576 | tf_op jit(solution)/shard_map/all_to_all | solution.py:203
  58.1 0.1 copy.14
  58.1 0.6 reshape_squeeze.3.lay_ref
  58.7 0.0 copy-done
  58.7 9.7 %shard_map.94 = (bf16[16,128,128]{2,1,0:T(8,128)(2,1)}, f32[16,128,512]{2,1,0:T(8,128)}) custom-call(s32[64]{0:T(128)} %reshape_squeeze.3.lay_ref, s32[16]{0:T(128)} %bitcast.7, bf16[16,3,128,128]{3,2,1,0:T(8,128)(2,1)} %copy-done), custom_call_target="tpu_custom_call" | custom-call | flops 536870912 | bytes 6291456 | tf_op jit(solution)/shard_map/pallas_call | solution.py:106
  68.5 6.8 %all-to-all-done.2 = bf16[16,1,128,128]{3,2,1,0:T(8,128)(2,1)S(1)} async-done(((bf16[16,1,128,128]{3,2,1,0:T(8,128)(2,1)}), bf16[16,1,128,128]{3,2,1,0:T(8,128)(2,1)S(1)}, u32[]{:S(2)}, u32[]{:S(2)}) %all-to-all-start.2) | async-done | bytes 524320 | tf_op jit(solution)/shard_map/all_to_all | solution.py:203
  75.3 3.5 %all-to-all-start.1 = ((bf16[16,128,128]{2,1,0:T(8,128)(2,1)}), bf16[16,128,128]{2,1,0:T(8,128)(2,1)S(1)}, u32[]{:S(2)}, u32[]{:S(2)}) async-start(bf16[16,128,128]{2,1,0:T(8,128)(2,1)} %get-tuple-element.9.o_ref), calls=%async_computation.1 | async-start | bytes 1048576 | tf_op jit(solution)/shard_map/all_to_all | solution.py:208
  78.7 9.6 %shard_map.97 = bf16[16,3,128,128]{3,2,1,0:T(8,128)(2,1)} custom-call(s32[64]{0:T(128)} %reshape_squeeze.3.lay_ref, bf16[16,3,128,128]{3,2,1,0:T(8,128)(2,1)} %copy-done, bf16[16,128,128]{2,1,0:T(8,128)(2,1)} %bitcast.5, bf16[16,128,128]{2,1,0:T(8,128)(2,1)} %get-tuple-element.9.o_ref, f32[16,128,512]{2,1,0:T(8,128)} %get-tuple-element.10.w_ref), custom_call_target="tpu_custom_call" | custom-call | flops 1073741824 | bytes 8912896 | tf_op jit(solution)/shard_map/pallas_call | solution.py:130
  88.4 7.0 %all-to-all-done.1 = bf16[16,128,128]{2,1,0:T(8,128)(2,1)S(1)} async-done(((bf16[16,128,128]{2,1,0:T(8,128)(2,1)}), bf16[16,128,128]{2,1,0:T(8,128)(2,1)S(1)}, u32[]{:S(2)}, u32[]{:S(2)}) %all-to-all-start.1) | async-done | bytes 524320 | tf_op jit(solution)/shard_map/all_to_all | solution.py:208
  95.4 0.8 copy-done.3
  96.2 3.6 %all-to-all-start.3 = ((bf16[16,3,128,128]{3,2,1,0:T(8,128)(2,1)}), bf16[16,3,128,128]{3,2,1,0:T(8,128)(2,1)S(1)}, u32[]{:S(2)}, u32[]{:S(2)}) async-start(bf16[16,3,128,128]{3,2,1,0:T(8,128)(2,1)} %shard_map.97), calls=%async_computation.3 | async-start | bytes 3145728 | tf_op jit(solution)/shard_map/all_to_all | solution.py:210
  99.8 2.0 %shard_map.95 = bf16[1,128,2048]{2,1,0:T(8,128)(2,1)} custom-call(bf16[16,1,128,128]{3,2,1,0:T(8,128)(2,1)} %bitcast.6), custom_call_target="tpu_custom_call" | custom-call | bytes 1048576 | tf_op jit(solution)/shard_map/pallas_call | solution.py:186
  101.8 35.9 %all-to-all-done.3.back_ref = bf16[16,3,128,128]{3,2,1,0:T(8,128)(2,1)S(1)} async-done(((bf16[16,3,128,128]{3,2,1,0:T(8,128)(2,1)}), bf16[16,3,128,128]{3,2,1,0:T(8,128)(2,1)S(1)}, u32[]{:S(2)}, u32[]{:S(2)}) %all-to-all-start.3) | async-done | bytes 1572896 | tf_op jit(solution)/shard_map/all_to_all | solution.py:210
  137.7 1.2 copy-done.1
  138.9 3.0 %shard_map.98 = (bf16[1,128,2048]{2,1,0:T(8,128)(2,1)}, bf16[1,128,2048]{2,1,0:T(8,128)(2,1)}, bf16[1,128,2048]{2,1,0:T(8,128)(2,1)}) custom-call(bf16[16,3,128,128]{3,2,1,0:T(8,128)(2,1)} %copy-done.1), custom_call_target="tpu_custom_call" | custom-call | bytes 3145728 | tf_op jit(solution)/shard_map/pallas_call | solution.py:186
  (8 shorter events, 0.0 us)
Async XLA Ops:
  3.4 12.0 %copy-start.6 = (bf16[1,128,2048]{2,1,0:T(8,128)(2,1)S(1)}, bf16[1,128,2048]{2,1,0:T(8,128)(2,1)}, u32[]{:S(2)}) copy-start(bf16[1,128,2048]{2,1,0:T(8,128)(2,1)} %param.9) | copy-start | bytes 1572868
  3.4 50.5 %all-to-all-start = ((bf16[16,3,128,128]{3,2,1,0:T(8,128)(2,1)}), bf16[16,3,128,128]{3,2,1,0:T(8,128)(2,1)S(1)}, u32[]{:S(2)}, u32[]{:S(2)}) async-start(bf16[16,3,128,128]{3,2,1,0:T(8,128)(2,1)} %shard_map.93), calls=%async_computation | async-start | bytes 3145728 | tf_op jit(solution)/shard_map/all_to_all | solution.py:200
  15.4 42.7 %copy-start.5 = (s32[1,1,16,4]{2,3,1,0:T(4,128)S(1)}, s32[1,1,16,4]{2,3,1,0:T(4,128)}, u32[]{:S(2)}) copy-start(s32[1,1,16,4]{2,3,1,0:T(4,128)} %param.10) | copy-start | bytes 772
  15.4 18.5 %collective-permute-start = (bf16[1,128,2048]{2,1,0:T(8,128)(2,1)S(1)}, bf16[1,128,2048]{2,1,0:T(8,128)(2,1)S(1)}, u32[]{:S(2)}, u32[]{:S(2)}) collective-permute-start(bf16[1,128,2048]{2,1,0:T(8,128)(2,1)S(1)} %copy-done.6), channel_id=1, source_target_pairs={{0,496},{16,0},{32,16},{48,32},{64,48},{80,64},{96,80},{112,96},{1... | collective-permute-start | bytes 1572872 | tf_op jit(solution)/shard_map/ppermute | solution.py:19
  33.9 0.8 copy-start.4
  53.9 4.8 %copy-start = (bf16[16,3,128,128]{3,2,1,0:T(8,128)(2,1)}, bf16[16,3,128,128]{3,2,1,0:T(8,128)(2,1)S(1)}, u32[]{:S(2)}) copy-start(bf16[16,3,128,128]{3,2,1,0:T(8,128)(2,1)S(1)} %all-to-all-done.qkv_ref) | copy-start | bytes 4718596
  53.9 21.3 %all-to-all-start.2 = ((bf16[16,1,128,128]{3,2,1,0:T(8,128)(2,1)}), bf16[16,1,128,128]{3,2,1,0:T(8,128)(2,1)S(1)}, u32[]{:S(2)}, u32[]{:S(2)}) async-start(bf16[16,1,128,128]{3,2,1,0:T(8,128)(2,1)} %shard_map.96), calls=%async_computation.2 | async-start | bytes 1048576 | tf_op jit(solution)/shard_map/all_to_all | solution.py:203
  75.3 3.5 %copy-start.2 = (bf16[16,1,128,128]{3,2,1,0:T(8,128)(2,1)}, bf16[16,1,128,128]{3,2,1,0:T(8,128)(2,1)S(1)}, u32[]{:S(2)}) copy-start(bf16[16,1,128,128]{3,2,1,0:T(8,128)(2,1)S(1)} %all-to-all-done.2) | copy-start | bytes 1572868
  75.3 20.2 %all-to-all-start.1 = ((bf16[16,128,128]{2,1,0:T(8,128)(2,1)}), bf16[16,128,128]{2,1,0:T(8,128)(2,1)S(1)}, u32[]{:S(2)}, u32[]{:S(2)}) async-start(bf16[16,128,128]{2,1,0:T(8,128)(2,1)} %get-tuple-element.9.o_ref), calls=%async_computation.1 | async-start | bytes 1048576 | tf_op jit(solution)/shard_map/all_to_all | solution.py:208
  95.4 0.8 copy-start.3
  96.2 41.5 %all-to-all-start.3 = ((bf16[16,3,128,128]{3,2,1,0:T(8,128)(2,1)}), bf16[16,3,128,128]{3,2,1,0:T(8,128)(2,1)S(1)}, u32[]{:S(2)}, u32[]{:S(2)}) async-start(bf16[16,3,128,128]{3,2,1,0:T(8,128)(2,1)} %shard_map.97), calls=%async_computation.3 | async-start | bytes 3145728 | tf_op jit(solution)/shard_map/all_to_all | solution.py:210
  137.7 1.2 copy-start.1

commit v5 on v4

--- a/solution.py
+++ b/solution.py
@@ -82,7 +82,8 @@
         )
         grad_score = (weights * (grad_weight - row_inner)).astype(jnp.bfloat16)
         grad_query = jnp.dot(grad_score, key_rows, preferred_element_type=jnp.float32)
-        out_ref[a, 0] = (grad_query * score_scale).astype(jnp.bfloat16)
+        out_ref[a, 0] = o_ref[a]
+        out_ref[a, 1] = (grad_query * score_scale).astype(jnp.bfloat16)
         grad_key_rows = lax.dot_general(
             grad_score, q, (((0,), (0,)), ((), ())), preferred_element_type=jnp.float32
         ) * score_scale
@@ -96,8 +97,8 @@
 
     lax.fori_loop(0, block_count, body, 0, unroll=4)
     for b in range(block_count):
-        out_ref[b, 1] = dk_acc[b].astype(jnp.bfloat16)
-        out_ref[b, 2] = dv_acc[b].astype(jnp.bfloat16)
+        out_ref[b, 2] = dk_acc[b].astype(jnp.bfloat16)
+        out_ref[b, 3] = dv_acc[b].astype(jnp.bfloat16)
 
 
 def forward_pass(plan, documents, qkv):
@@ -129,7 +130,7 @@
     flops = 4 * 2 * block_count * rows * SLOTS * rows * head_dim
     return pl.pallas_call(
         backward_kernel,
-        out_shape=jax.ShapeDtypeStruct((block_count, 3, rows, head_dim), jnp.bfloat16),
+        out_shape=jax.ShapeDtypeStruct((block_count, 4, rows, head_dim), jnp.bfloat16),
         in_specs=[pl.BlockSpec(memory_space=pltpu.SMEM)]
         + [pl.BlockSpec(memory_space=pltpu.VMEM)] * 4,
         out_specs=pl.BlockSpec(memory_space=pltpu.VMEM),
@@ -205,11 +206,9 @@
     plan = layout[0, 0].reshape(block_count * SLOTS)
     documents = segments[0]
     attended, weights = forward_pass(plan, documents, fields)
-    attended_back = lax.all_to_all(attended, "ctx", 0, 0, tiled=True)
     results = backward_pass(plan, fields, grad, attended, weights)
     back = lax.all_to_all(results, "ctx", 0, 0, tiled=True)
-    (attended_out,) = unshuffle(attended_back[:, None], section_rows)
-    return (attended_out, *unshuffle(back, section_rows))
+    return tuple(unshuffle(back, section_rows))
 
 
 def solution(mesh):

time: 142 us -> 144 us (1.014)
  blocking collectives: 0 us -> 54 us
  waiting for transfers between devices: 78.2 us -> 35.3 us
  starting transfers between devices: 30.5 us -> 23.4 us
    all_to_all x0 -> x1, blocking collectives: none -> 54 us  [local(): back = lax.all_to_all(results, 'ctx', 0, 0, tiled=True)]
    all_to_all x2 -> x0, waiting for transfers between devices: 42.9 us -> none  [the longest x1 35.9 us: local(): back = lax.all_to_all(results, 'ctx', 0, 0, tiled=True)]
    all_to_all x2 -> x0, starting transfers between devices: 7.08 us -> none  [the longest x1 3.6 us: local(): back = lax.all_to_all(results, 'ctx', 0, 0, tiled=True)]
    pallas_call x2 -> x1, Pallas kernels: 4.92 us -> 3.45 us  [unshuffle(): pl.pallas_call(unshuffle_kernel, out_shape=[field] * arrays, in_specs=[pl...]
  transfers between devices with their start and end apart: 5 -> 3, of which waited for: 5 -> 3; matrix products, arithmetic and copies ran while one was open for 0% -> 0% of each run, Pallas kernels for 16% -> 8%
where the time goes in v5:
time: 144 us; the launch traced here: 143 us
  blocking collectives  54 us (38%)
  waiting for transfers between devices  35.3 us (25%)
  Pallas kernels  27.7 us (19%)
  starting transfers between devices  23.4 us (16%)
  local copies, waits for them, and re-layouts  2.28 us (2%)
    all_to_all x1, blocking collectives, local(): back = lax.all_to_all(results, 'ctx', 0, 0, tiled=True)  54 us
    all_to_all x1, waiting for transfers between devices, local(): fields = lax.all_to_all(fields, 'ctx', 0, 0, tiled=True)  17.3 us
    all_to_all x1, starting transfers between devices, local(): fields = lax.all_to_all(fields, 'ctx', 0, 0, tiled=True)  12 us
    ppermute x1, waiting for transfers between devices, passed_along(): return lax.ppermute(value, axis, pairs)  11.2 us
    pallas_call x1, Pallas kernels, backward_pass(): pl.pallas_call(backward_kernel, out_shape=jax.ShapeDtypeStruct((block_cou...  9.8 us
    pallas_call x1, Pallas kernels, forward_pass(): pl.pallas_call(forward_kernel, out_shape=[jax.ShapeDtypeStruct((block_cou...  9.71 us
    ppermute x1, starting transfers between devices, passed_along(): return lax.ppermute(value, axis, pairs)  7.29 us
    all_to_all x1, waiting for transfers between devices, local(): grad = lax.all_to_all(grad, 'ctx', 0, 0, tiled=True)[:, 0]  6.8 us
  transfers between devices with their start and end apart: 3, of which 3 were waited for; matrix products, arithmetic and copies ran while one was open for 0% of the time, Pallas kernels for 8%

profile of v5, /device:TPU:1, one launch (start us, length us, event | category | flops | bytes accessed | tf_op | source)
XLA Modules:
  0.0 143.3 jit_solution(3100084505973613908)
XLA Ops:
  0.6 2.8 %shard_map.93 = bf16[16,3,128,128]{3,2,1,0:T(8,128)(2,1)} custom-call(bf16[1,128,2048]{2,1,0:T(8,128)(2,1)} %refs_0_.1, bf16[1,128,2048]{2,1,0:T(8,128)(2,1)} %refs_1_.1, bf16[1,128,2048]{2,1,0:T(8,128)(2,1)} %refs_2_.1), custom_call_target="tpu_custom_call" | custom-call | bytes 3145728 | tf_op jit(solution)/shard_map/pallas_call | solution.py:163
  3.4 0.0 copy-start.4
  3.4 0.0 copy-start.3
  3.4 12.0 %all-to-all-start = ((bf16[16,3,128,128]{3,2,1,0:T(8,128)(2,1)}), bf16[16,3,128,128]{3,2,1,0:T(8,128)(2,1)S(1)}, u32[]{:S(2)}, u32[]{:S(2)}) async-start(bf16[16,3,128,128]{3,2,1,0:T(8,128)(2,1)} %shard_map.93), calls=%async_computation | async-start | bytes 3145728 | tf_op jit(solution)/shard_map/all_to_all | solution.py:201
  15.4 0.0 copy-done.4
  15.4 7.3 %collective-permute-start = (bf16[1,128,2048]{2,1,0:T(8,128)(2,1)S(1)}, bf16[1,128,2048]{2,1,0:T(8,128)(2,1)S(1)}, u32[]{:S(2)}, u32[]{:S(2)}) collective-permute-start(bf16[1,128,2048]{2,1,0:T(8,128)(2,1)S(1)} %copy-done.4), channel_id=1, source_target_pairs={{0,496},{16,0},{32,16},{48,32},{64,48},{80,64},{96,80},{112,96},{1... | collective-permute-start | bytes 1572872 | tf_op jit(solution)/shard_map/ppermute | solution.py:19
  22.7 11.2 %collective-permute-done.refs_0_ = bf16[1,128,2048]{2,1,0:T(8,128)(2,1)S(1)} collective-permute-done((bf16[1,128,2048]{2,1,0:T(8,128)(2,1)S(1)}, bf16[1,128,2048]{2,1,0:T(8,128)(2,1)S(1)}, u32[]{:S(2)}, u32[]{:S(2)}) %collective-permute-start) | collective-permute-done | bytes 524320 | tf_op jit(solution)/shard_map/ppermute | solution.py:19
  33.8 0.0 copy-start.2
  33.8 0.8 copy-done.2
  34.6 1.9 %shard_map.94 = bf16[16,1,128,128]{3,2,1,0:T(8,128)(2,1)} custom-call(bf16[1,128,2048]{2,1,0:T(8,128)(2,1)} %copy-done.2), custom_call_target="tpu_custom_call" | custom-call | bytes 1048576 | tf_op jit(solution)/shard_map/pallas_call | solution.py:163
  36.6 17.3 %all-to-all-done.qkv_ref = bf16[16,3,128,128]{3,2,1,0:T(8,128)(2,1)S(1)} async-done(((bf16[16,3,128,128]{3,2,1,0:T(8,128)(2,1)}), bf16[16,3,128,128]{3,2,1,0:T(8,128)(2,1)S(1)}, u32[]{:S(2)}, u32[]{:S(2)}) %all-to-all-start) | async-done | bytes 1572896 | tf_op jit(solution)/shard_map/all_to_all | solution.py:201
  53.9 0.0 copy-start
  53.9 4.1 %all-to-all-start.1 = ((bf16[16,1,128,128]{3,2,1,0:T(8,128)(2,1)}), bf16[16,1,128,128]{3,2,1,0:T(8,128)(2,1)S(1)}, u32[]{:S(2)}, u32[]{:S(2)}) async-start(bf16[16,1,128,128]{3,2,1,0:T(8,128)(2,1)} %shard_map.94), calls=%async_computation.1 | async-start | bytes 1048576 | tf_op jit(solution)/shard_map/all_to_all | solution.py:204
  58.0 0.0 copy-done.3
  58.0 0.1 copy.14
  58.1 0.6 reshape_squeeze.3.lay_ref
  58.7 0.0 copy-done
  58.7 9.7 %shard_map.95 = (bf16[16,128,128]{2,1,0:T(8,128)(2,1)}, f32[16,128,512]{2,1,0:T(8,128)}) custom-call(s32[64]{0:T(128)} %reshape_squeeze.3.lay_ref, s32[16]{0:T(128)} %bitcast.5, bf16[16,3,128,128]{3,2,1,0:T(8,128)(2,1)} %copy-done), custom_call_target="tpu_custom_call" | custom-call | flops 536870912 | bytes 6291456 | tf_op jit(solution)/shard_map/pallas_call | solution.py:107
  68.4 6.8 %all-to-all-done.1 = bf16[16,1,128,128]{3,2,1,0:T(8,128)(2,1)S(1)} async-done(((bf16[16,1,128,128]{3,2,1,0:T(8,128)(2,1)}), bf16[16,1,128,128]{3,2,1,0:T(8,128)(2,1)S(1)}, u32[]{:S(2)}, u32[]{:S(2)}) %all-to-all-start.1) | async-done | bytes 524320 | tf_op jit(solution)/shard_map/all_to_all | solution.py:204
  75.2 0.0 copy-start.1
  75.2 0.8 copy-done.1
  76.0 9.8 %shard_map.96 = bf16[16,4,128,128]{3,2,1,0:T(8,128)(2,1)} custom-call(s32[64]{0:T(128)} %reshape_squeeze.3.lay_ref, bf16[16,3,128,128]{3,2,1,0:T(8,128)(2,1)} %copy-done, bf16[16,128,128]{2,1,0:T(8,128)(2,1)} %bitcast.4, bf16[16,128,128]{2,1,0:T(8,128)(2,1)} %get-tuple-element.6.o_ref, f32[16,128,512]{2,1,0:T(8,128)} %get-tuple-element.7.w_ref), custom_call_target="tpu_custom_call" | custom-call | flops 1073741824 | bytes 8912896 | tf_op jit(solution)/shard_map/pallas_call | solution.py:131
  85.8 54.0 %all_to_all.15.back_ref = bf16[16,4,128,128]{3,2,1,0:T(8,128)(2,1)} all-to-all(bf16[16,4,128,128]{3,2,1,0:T(8,128)(2,1)} %shard_map.96), channel_id=1, replica_groups=mesh['section'=32,'ctx'=16] {'ctx'}, dimensions={0} | all-to-all | bytes 4194304 | tf_op jit(solution)/shard_map/all_to_all | solution.py:210
  139.8 3.4 %shard_map.97 = (bf16[1,128,2048]{2,1,0:T(8,128)(2,1)}, bf16[1,128,2048]{2,1,0:T(8,128)(2,1)}, bf16[1,128,2048]{2,1,0:T(8,128)(2,1)}, bf16[1,128,2048]{2,1,0:T(8,128)(2,1)}) custom-call(bf16[16,4,128,128]{3,2,1,0:T(8,128)(2,1)} %all_to_all.15.back_ref), custom_call_target="tpu_custom_call" | custom-call | bytes 4194304 | tf_op jit(solution)/shard_map/pallas_call | solution.py:187
Async XLA Ops:
  3.4 12.0 %copy-start.4 = (bf16[1,128,2048]{2,1,0:T(8,128)(2,1)S(1)}, bf16[1,128,2048]{2,1,0:T(8,128)(2,1)}, u32[]{:S(2)}) copy-start(bf16[1,128,2048]{2,1,0:T(8,128)(2,1)} %param.9) | copy-start | bytes 1572868
  3.4 54.6 %copy-start.3 = (s32[1,1,16,4]{2,3,1,0:T(4,128)S(1)}, s32[1,1,16,4]{2,3,1,0:T(4,128)}, u32[]{:S(2)}) copy-start(s32[1,1,16,4]{2,3,1,0:T(4,128)} %param.10) | copy-start | bytes 772
  3.4 50.5 %all-to-all-start = ((bf16[16,3,128,128]{3,2,1,0:T(8,128)(2,1)}), bf16[16,3,128,128]{3,2,1,0:T(8,128)(2,1)S(1)}, u32[]{:S(2)}, u32[]{:S(2)}) async-start(bf16[16,3,128,128]{3,2,1,0:T(8,128)(2,1)} %shard_map.93), calls=%async_computation | async-start | bytes 3145728 | tf_op jit(solution)/shard_map/all_to_all | solution.py:201
  15.4 18.5 %collective-permute-start = (bf16[1,128,2048]{2,1,0:T(8,128)(2,1)S(1)}, bf16[1,128,2048]{2,1,0:T(8,128)(2,1)S(1)}, u32[]{:S(2)}, u32[]{:S(2)}) collective-permute-start(bf16[1,128,2048]{2,1,0:T(8,128)(2,1)S(1)} %copy-done.4), channel_id=1, source_target_pairs={{0,496},{16,0},{32,16},{48,32},{64,48},{80,64},{96,80},{112,96},{1... | collective-permute-start | bytes 1572872 | tf_op jit(solution)/shard_map/ppermute | solution.py:19
  33.8 0.8 copy-start.2
  53.9 4.8 %copy-start = (bf16[16,3,128,128]{3,2,1,0:T(8,128)(2,1)}, bf16[16,3,128,128]{3,2,1,0:T(8,128)(2,1)S(1)}, u32[]{:S(2)}) copy-start(bf16[16,3,128,128]{3,2,1,0:T(8,128)(2,1)S(1)} %all-to-all-done.qkv_ref) | copy-start | bytes 4718596
  53.9 21.3 %all-to-all-start.1 = ((bf16[16,1,128,128]{3,2,1,0:T(8,128)(2,1)}), bf16[16,1,128,128]{3,2,1,0:T(8,128)(2,1)S(1)}, u32[]{:S(2)}, u32[]{:S(2)}) async-start(bf16[16,1,128,128]{3,2,1,0:T(8,128)(2,1)} %shard_map.94), calls=%async_computation.1 | async-start | bytes 1048576 | tf_op jit(solution)/shard_map/all_to_all | solution.py:204
  75.2 0.8 copy-start.1

commit v6 on v4

--- a/solution.py
+++ b/solution.py
@@ -172,12 +172,20 @@
     )(*fields)
 
 
-def unshuffle_kernel(back_ref, *out_refs):
-    head_count = back_ref.shape[0]
-    head_dim = back_ref.shape[-1]
-    for i, out_ref in enumerate(out_refs):
-        for h in range(head_count):
-            out_ref[0, :, h * head_dim:(h + 1) * head_dim] = back_ref[h, i]
+def unshuffle_kernel(back_hbm, *refs):
+    *out_refs, buf, sems = refs
+    head_count = back_hbm.shape[0]
+    head_dim = back_hbm.shape[-1]
+    copies = [
+        pltpu.make_async_copy(back_hbm.at[h], buf.at[h], sems.at[h])
+        for h in range(head_count)
+    ]
+    for copy in copies:
+        copy.start()
+    for h, copy in enumerate(copies):
+        copy.wait()
+        for i, out_ref in enumerate(out_refs):
+            out_ref[0, :, h * head_dim:(h + 1) * head_dim] = buf[h, i]
 
 
 def unshuffle(back, section_rows):
@@ -186,8 +194,12 @@
     return pl.pallas_call(
         unshuffle_kernel,
         out_shape=[field] * arrays,
-        in_specs=[pl.BlockSpec(memory_space=pltpu.VMEM)],
+        in_specs=[pl.BlockSpec(memory_space=pl.ANY)],
         out_specs=[pl.BlockSpec(memory_space=pltpu.VMEM)] * arrays,
+        scratch_shapes=[
+            pltpu.VMEM(back.shape, back.dtype),
+            pltpu.SemaphoreType.DMA((head_count,)),
+        ],
         cost_estimate=pl.CostEstimate(
             flops=0, transcendentals=0, bytes_accessed=4 * back.size
         ),

time: 142 us -> 142 us (level)
  no operation moved by 1% of the time
where the time goes in v6:
time: 142 us
  waiting for transfers between devices  78.2 us (55%)
  starting transfers between devices  30.5 us (21%)
  Pallas kernels  28.8 us (20%)
  local copies, waits for them, and re-layouts  3.46 us (2%)
    all_to_all x1, waiting for transfers between devices, local(): back = lax.all_to_all(results, 'ctx', 0, 0, tiled=True)  35.9 us
    all_to_all x1, waiting for transfers between devices, local(): fields = lax.all_to_all(fields, 'ctx', 0, 0, tiled=True)  17.3 us
    all_to_all x1, starting transfers between devices, local(): fields = lax.all_to_all(fields, 'ctx', 0, 0, tiled=True)  12 us
    ppermute x1, waiting for transfers between devices, passed_along(): return lax.ppermute(value, axis, pairs)  11.2 us
    pallas_call x1, Pallas kernels, forward_pass(): pl.pallas_call(forward_kernel, out_shape=[jax.ShapeDtypeStruct((block_cou...  9.72 us
    pallas_call x1, Pallas kernels, backward_pass(): pl.pallas_call(backward_kernel, out_shape=jax.ShapeDtypeStruct((block_cou...  9.65 us
    ppermute x1, starting transfers between devices, passed_along(): return lax.ppermute(value, axis, pairs)  7.29 us
    all_to_all x1, waiting for transfers between devices, local(): attended_back = lax.all_to_all(attended, 'ctx', 0, 0, tiled=True)  7.03 us
  transfers between devices with their start and end apart: 5, of which 5 were waited for; matrix products, arithmetic and copies ran while one was open for 0% of the time, Pallas kernels for 16%

profile of v6, /device:TPU:1, one launch (start us, length us, event | category | flops | bytes accessed | tf_op | source)
XLA Modules:
  0.0 141.6 jit_solution(8914717137680372756)
XLA Ops:
  0.6 2.8 %shard_map.93 = bf16[16,3,128,128]{3,2,1,0:T(8,128)(2,1)} custom-call(bf16[1,128,2048]{2,1,0:T(8,128)(2,1)} %refs_0_.1, bf16[1,128,2048]{2,1,0:T(8,128)(2,1)} %refs_1_.1, bf16[1,128,2048]{2,1,0:T(8,128)(2,1)} %refs_2_.1), custom_call_target="tpu_custom_call" | custom-call | bytes 3145728 | tf_op jit(solution)/shard_map/pallas_call | solution.py:162
  3.4 12.0 %all-to-all-start = ((bf16[16,3,128,128]{3,2,1,0:T(8,128)(2,1)}), bf16[16,3,128,128]{3,2,1,0:T(8,128)(2,1)S(1)}, u32[]{:S(2)}, u32[]{:S(2)}) async-start(bf16[16,3,128,128]{3,2,1,0:T(8,128)(2,1)} %shard_map.93), calls=%async_computation | async-start | bytes 3145728 | tf_op jit(solution)/shard_map/all_to_all | solution.py:212
  15.4 0.0 copy-done.6
  15.4 0.0 copy-start.5
  15.4 7.3 %collective-permute-start = (bf16[1,128,2048]{2,1,0:T(8,128)(2,1)S(1)}, bf16[1,128,2048]{2,1,0:T(8,128)(2,1)S(1)}, u32[]{:S(2)}, u32[]{:S(2)}) collective-permute-start(bf16[1,128,2048]{2,1,0:T(8,128)(2,1)S(1)} %copy-done.6), channel_id=1, source_target_pairs={{0,496},{16,0},{32,16},{48,32},{64,48},{80,64},{96,80},{112,96},{1... | collective-permute-start | bytes 1572872 | tf_op jit(solution)/shard_map/ppermute | solution.py:19
  22.7 11.2 %collective-permute-done.refs_0_ = bf16[1,128,2048]{2,1,0:T(8,128)(2,1)S(1)} collective-permute-done((bf16[1,128,2048]{2,1,0:T(8,128)(2,1)S(1)}, bf16[1,128,2048]{2,1,0:T(8,128)(2,1)S(1)}, u32[]{:S(2)}, u32[]{:S(2)}) %collective-permute-start) | collective-permute-done | bytes 524320 | tf_op jit(solution)/shard_map/ppermute | solution.py:19
  33.9 0.8 copy-done.4
  34.7 1.9 %shard_map.96 = bf16[16,1,128,128]{3,2,1,0:T(8,128)(2,1)} custom-call(bf16[1,128,2048]{2,1,0:T(8,128)(2,1)} %copy-done.4), custom_call_target="tpu_custom_call" | custom-call | bytes 1048576 | tf_op jit(solution)/shard_map/pallas_call | solution.py:162
  36.6 17.3 %all-to-all-done.qkv_ref = bf16[16,3,128,128]{3,2,1,0:T(8,128)(2,1)S(1)} async-done(((bf16[16,3,128,128]{3,2,1,0:T(8,128)(2,1)}), bf16[16,3,128,128]{3,2,1,0:T(8,128)(2,1)S(1)}, u32[]{:S(2)}, u32[]{:S(2)}) %all-to-all-start) | async-done | bytes 1572896 | tf_op jit(solution)/shard_map/all_to_all | solution.py:212
  53.9 4.1 %all-to-all-start.2 = ((bf16[16,1,128,128]{3,2,1,0:T(8,128)(2,1)}), bf16[16,1,128,128]{3,2,1,0:T(8,128)(2,1)S(1)}, u32[]{:S(2)}, u32[]{:S(2)}) async-start(bf16[16,1,128,128]{3,2,1,0:T(8,128)(2,1)} %shard_map.96), calls=%async_computation.2 | async-start | bytes 1048576 | tf_op jit(solution)/shard_map/all_to_all | solution.py:215
  58.1 0.1 copy.14
  58.1 0.6 reshape_squeeze.3.lay_ref
  58.7 0.0 copy-done
  58.7 9.7 %shard_map.94 = (bf16[16,128,128]{2,1,0:T(8,128)(2,1)}, f32[16,128,512]{2,1,0:T(8,128)}) custom-call(s32[64]{0:T(128)} %reshape_squeeze.3.lay_ref, s32[16]{0:T(128)} %bitcast.7, bf16[16,3,128,128]{3,2,1,0:T(8,128)(2,1)} %copy-done), custom_call_target="tpu_custom_call" | custom-call | flops 536870912 | bytes 6291456 | tf_op jit(solution)/shard_map/pallas_call | solution.py:106
  68.5 6.8 %all-to-all-done.2 = bf16[16,1,128,128]{3,2,1,0:T(8,128)(2,1)S(1)} async-done(((bf16[16,1,128,128]{3,2,1,0:T(8,128)(2,1)}), bf16[16,1,128,128]{3,2,1,0:T(8,128)(2,1)S(1)}, u32[]{:S(2)}, u32[]{:S(2)}) %all-to-all-start.2) | async-done | bytes 524320 | tf_op jit(solution)/shard_map/all_to_all | solution.py:215
  75.3 3.5 %all-to-all-start.1 = ((bf16[16,128,128]{2,1,0:T(8,128)(2,1)}), bf16[16,128,128]{2,1,0:T(8,128)(2,1)S(1)}, u32[]{:S(2)}, u32[]{:S(2)}) async-start(bf16[16,128,128]{2,1,0:T(8,128)(2,1)} %get-tuple-element.9.o_ref), calls=%async_computation.1 | async-start | bytes 1048576 | tf_op jit(solution)/shard_map/all_to_all | solution.py:220
  78.7 9.6 %shard_map.97 = bf16[16,3,128,128]{3,2,1,0:T(8,128)(2,1)} custom-call(s32[64]{0:T(128)} %reshape_squeeze.3.lay_ref, bf16[16,3,128,128]{3,2,1,0:T(8,128)(2,1)} %copy-done, bf16[16,128,128]{2,1,0:T(8,128)(2,1)} %bitcast.5, bf16[16,128,128]{2,1,0:T(8,128)(2,1)} %get-tuple-element.9.o_ref, f32[16,128,512]{2,1,0:T(8,128)} %get-tuple-element.10.w_ref), custom_call_target="tpu_custom_call" | custom-call | flops 1073741824 | bytes 8912896 | tf_op jit(solution)/shard_map/pallas_call | solution.py:130
  88.4 7.0 %all-to-all-done.1 = bf16[16,128,128]{2,1,0:T(8,128)(2,1)S(1)} async-done(((bf16[16,128,128]{2,1,0:T(8,128)(2,1)}), bf16[16,128,128]{2,1,0:T(8,128)(2,1)S(1)}, u32[]{:S(2)}, u32[]{:S(2)}) %all-to-all-start.1) | async-done | bytes 524320 | tf_op jit(solution)/shard_map/all_to_all | solution.py:220
  95.4 0.8 copy-done.3
  96.2 3.6 %all-to-all-start.3 = ((bf16[16,3,128,128]{3,2,1,0:T(8,128)(2,1)}), bf16[16,3,128,128]{3,2,1,0:T(8,128)(2,1)S(1)}, u32[]{:S(2)}, u32[]{:S(2)}) async-start(bf16[16,3,128,128]{3,2,1,0:T(8,128)(2,1)} %shard_map.97), calls=%async_computation.3 | async-start | bytes 3145728 | tf_op jit(solution)/shard_map/all_to_all | solution.py:222
  99.8 1.9 %shard_map.95 = bf16[1,128,2048]{2,1,0:T(8,128)(2,1)} custom-call(bf16[16,1,128,128]{3,2,1,0:T(8,128)(2,1)} %bitcast.6), custom_call_target="tpu_custom_call" | custom-call | bytes 1048576 | tf_op jit(solution)/shard_map/pallas_call | solution.py:194
  101.8 35.9 %all-to-all-done.3.back_hbm = bf16[16,3,128,128]{3,2,1,0:T(8,128)(2,1)S(1)} async-done(((bf16[16,3,128,128]{3,2,1,0:T(8,128)(2,1)}), bf16[16,3,128,128]{3,2,1,0:T(8,128)(2,1)S(1)}, u32[]{:S(2)}, u32[]{:S(2)}) %all-to-all-start.3) | async-done | bytes 1572896 | tf_op jit(solution)/shard_map/all_to_all | solution.py:222
  137.7 1.2 copy-done.1
  138.9 2.8 %shard_map.98 = (bf16[1,128,2048]{2,1,0:T(8,128)(2,1)}, bf16[1,128,2048]{2,1,0:T(8,128)(2,1)}, bf16[1,128,2048]{2,1,0:T(8,128)(2,1)}) custom-call(bf16[16,3,128,128]{3,2,1,0:T(8,128)(2,1)} %copy-done.1), custom_call_target="tpu_custom_call" | custom-call | bytes 3145728 | tf_op jit(solution)/shard_map/pallas_call | solution.py:194
  (8 shorter events, 0.0 us)
Async XLA Ops:
  3.4 12.0 %copy-start.6 = (bf16[1,128,2048]{2,1,0:T(8,128)(2,1)S(1)}, bf16[1,128,2048]{2,1,0:T(8,128)(2,1)}, u32[]{:S(2)}) copy-start(bf16[1,128,2048]{2,1,0:T(8,128)(2,1)} %param.9) | copy-start | bytes 1572868
  3.4 50.5 %all-to-all-start = ((bf16[16,3,128,128]{3,2,1,0:T(8,128)(2,1)}), bf16[16,3,128,128]{3,2,1,0:T(8,128)(2,1)S(1)}, u32[]{:S(2)}, u32[]{:S(2)}) async-start(bf16[16,3,128,128]{3,2,1,0:T(8,128)(2,1)} %shard_map.93), calls=%async_computation | async-start | bytes 3145728 | tf_op jit(solution)/shard_map/all_to_all | solution.py:212
  15.4 42.7 %copy-start.5 = (s32[1,1,16,4]{2,3,1,0:T(4,128)S(1)}, s32[1,1,16,4]{2,3,1,0:T(4,128)}, u32[]{:S(2)}) copy-start(s32[1,1,16,4]{2,3,1,0:T(4,128)} %param.10) | copy-start | bytes 772
  15.4 18.5 %collective-permute-start = (bf16[1,128,2048]{2,1,0:T(8,128)(2,1)S(1)}, bf16[1,128,2048]{2,1,0:T(8,128)(2,1)S(1)}, u32[]{:S(2)}, u32[]{:S(2)}) collective-permute-start(bf16[1,128,2048]{2,1,0:T(8,128)(2,1)S(1)} %copy-done.6), channel_id=1, source_target_pairs={{0,496},{16,0},{32,16},{48,32},{64,48},{80,64},{96,80},{112,96},{1... | collective-permute-start | bytes 1572872 | tf_op jit(solution)/shard_map/ppermute | solution.py:19
  33.9 0.8 copy-start.4
  53.9 4.8 %copy-start = (bf16[16,3,128,128]{3,2,1,0:T(8,128)(2,1)}, bf16[16,3,128,128]{3,2,1,0:T(8,128)(2,1)S(1)}, u32[]{:S(2)}) copy-start(bf16[16,3,128,128]{3,2,1,0:T(8,128)(2,1)S(1)} %all-to-all-done.qkv_ref) | copy-start | bytes 4718596
  53.9 21.3 %all-to-all-start.2 = ((bf16[16,1,128,128]{3,2,1,0:T(8,128)(2,1)}), bf16[16,1,128,128]{3,2,1,0:T(8,128)(2,1)S(1)}, u32[]{:S(2)}, u32[]{:S(2)}) async-start(bf16[16,1,128,128]{3,2,1,0:T(8,128)(2,1)} %shard_map.96), calls=%async_computation.2 | async-start | bytes 1048576 | tf_op jit(solution)/shard_map/all_to_all | solution.py:215
  75.3 3.5 %copy-start.2 = (bf16[16,1,128,128]{3,2,1,0:T(8,128)(2,1)}, bf16[16,1,128,128]{3,2,1,0:T(8,128)(2,1)S(1)}, u32[]{:S(2)}) copy-start(bf16[16,1,128,128]{3,2,1,0:T(8,128)(2,1)S(1)} %all-to-all-done.2) | copy-start | bytes 1572868
  75.3 20.2 %all-to-all-start.1 = ((bf16[16,128,128]{2,1,0:T(8,128)(2,1)}), bf16[16,128,128]{2,1,0:T(8,128)(2,1)S(1)}, u32[]{:S(2)}, u32[]{:S(2)}) async-start(bf16[16,128,128]{2,1,0:T(8,128)(2,1)} %get-tuple-element.9.o_ref), calls=%async_computation.1 | async-start | bytes 1048576 | tf_op jit(solution)/shard_map/all_to_all | solution.py:220
  95.4 0.8 copy-start.3
  96.2 41.5 %all-to-all-start.3 = ((bf16[16,3,128,128]{3,2,1,0:T(8,128)(2,1)}), bf16[16,3,128,128]{3,2,1,0:T(8,128)(2,1)S(1)}, u32[]{:S(2)}, u32[]{:S(2)}) async-start(bf16[16,3,128,128]{3,2,1,0:T(8,128)(2,1)} %shard_map.97), calls=%async_computation.3 | async-start | bytes 3145728 | tf_op jit(solution)/shard_map/all_to_all | solution.py:222
  137.7 1.2 copy-start.1
